TPU v7x, 512 devices: a whole 4x8x8 slice. The times are simulated.
512 devices in a mesh: seq: 16 (over y, x_lo), chan: 32 (over z, x_hi, core).
Axes of the slice: x: 4 (x_hi: 2, x_lo: 2; x = x_hi * 2 + x_lo), y: 8, z: 8, core: 2. Of those that a mesh axis runs over, the one named last changes fastest.
Arguments:
- stream_in: bfloat16 [2048, 8192], P('seq', 'chan'), may hold values from -64 to 64
- outer_gate: bfloat16 [2048, 8192], P('seq', 'chan'), may hold values from -4 to 4
- inner_gate: bfloat16 [2048, 8192], P('seq', 'chan'), may hold values from -4 to 4
- values: bfloat16 [2048, 8192], P('seq', 'chan'), may hold values from -4 to 4
- long_filter: bfloat16 [2048, 8192], P('seq', 'chan'), may hold values from -1.2 to 1.2
- norm_gain: float32 [8192], P('chan'), may hold values from 0.5 to 1.5
- cotangent: bfloat16 [2048, 8192], P('seq', 'chan'), may hold values from -16 to 16
Outputs:
- normed: bfloat16 [2048, 8192], P('seq', 'chan')
- stream_grad: bfloat16 [2048, 8192], P('seq', 'chan')
- outer_grad: bfloat16 [2048, 8192], P('seq', 'chan')
- inner_grad: bfloat16 [2048, 8192], P('seq', 'chan')
- value_grad: bfloat16 [2048, 8192], P('seq', 'chan')
All inputs are finite; a program needn't handle non-finite values.
Results may differ from a plain program's by a relative error of at most 0.012.
Values may be sent and summed in bfloat16 or wider, within the bound.
No kernel may reach another device: no remote copies, remote signals or barrier semaphores. Data moves between devices by JAX's collectives and lax.ppermute only.
A program may use at most 64 MiB of HBM per device.

v0:
```python
import math

import jax
import jax.numpy as jnp
from jax import lax
from jax.sharding import PartitionSpec as P

EPSILON = 1e-06
HIGHEST_MODE = lax.Precision.HIGHEST


def from_behind(value, axis, steps):
    count = lax.axis_size(axis)
    first, last = (max(0, -steps), min(count, count - steps))
    return lax.ppermute(value, axis, [(source, source + steps) for source in range(first, last)])


def shortened(shard):

    def short(part):
        return part.astype(jnp.bfloat16) if part.dtype == jnp.float32 else part

    return jax.tree.map(short, shard)


def dft_tables(half):
    length = 2 * half
    rows = lax.broadcasted_iota(jnp.int32, (length, length), 0)
    cols = lax.broadcasted_iota(jnp.int32, (length, length), 1)
    step = math.pi / half
    phase = (rows % half * cols % length).astype(jnp.float32) * step
    nyquist = (half * cols % length).astype(jnp.float32) * step
    forward = jnp.where(
        rows < half, jnp.cos(phase), jnp.where(rows == half, jnp.cos(nyquist), -jnp.sin(phase))
    )
    phase_back = (cols % half * rows % length).astype(jnp.float32) * step
    nyquist_back = (half * rows % length).astype(jnp.float32) * step
    weight = jnp.where(cols == 0, 1.0, 2.0)
    inverse = jnp.where(
        cols < half,
        weight * jnp.cos(phase_back),
        jnp.where(cols == half, jnp.cos(nyquist_back), -2.0 * jnp.sin(phase_back)),
    )
    return (forward, inverse / length)


def spectral_product(left, right, conjugate):
    half = left.shape[-2] // 2
    left_real, left_imag = (left[..., :half, :], left[..., half:, :])
    right_real, right_imag = (right[..., :half, :], right[..., half:, :])
    first_bin = lax.broadcasted_iota(jnp.int32, (half, 1), 0) == 0
    if conjugate:
        right_eff = jnp.where(first_bin, right_imag, -right_imag)
    else:
        right_eff = right_imag
    real_out = left_real * right_real - jnp.where(first_bin, 0.0, left_imag * right_eff)
    imag_out = jnp.where(
        first_bin, left_imag * right_imag, left_real * right_eff + left_imag * right_real
    )
    return jnp.concatenate([real_out, imag_out], axis=-2)


def matmul_high(left, right):
    return jnp.dot(left, right, precision=HIGHEST_MODE, preferred_element_type=jnp.float32)


def body(stream_in, outer_gate, inner_gate, values, long_filter, norm_gain, cotangent):
    half = stream_in.shape[0]
    width = stream_in.shape[1]
    forward, inverse = dft_tables(half)
    forward_half = forward[:, :half]
    outer = outer_gate.astype(jnp.float32)
    inner = inner_gate.astype(jnp.float32)
    value_rows = values.astype(jnp.float32)
    token_position = lax.axis_index("seq")
    devices = lax.axis_size("seq")
    mixed = inner * value_rows
    data_spec = matmul_high(forward_half, mixed).astype(jnp.bfloat16)
    own_spec = matmul_high(forward_half, long_filter.astype(jnp.float32)).astype(jnp.bfloat16)
    filt_spec = lax.all_gather(own_spec[None], "seq", axis=0, tiled=True)
    zero_total = jnp.zeros((2 * half, width), jnp.float32)
    piece = lax.all_gather(data_spec[None], "seq", axis=0, tiled=True)

    def forward_one_block(offset, inner_total):
        lag = token_position - offset
        taps = lax.dynamic_index_in_dim(filt_spec, jnp.clip(lag, 0, devices - 1), 0, keepdims=False)
        block = lax.dynamic_index_in_dim(piece, offset, 0, keepdims=False)
        term = spectral_product(block.astype(jnp.float32), taps.astype(jnp.float32), False)
        return inner_total + jnp.where(lag >= 0, term, 0.0)

    total = lax.fori_loop(0, piece.shape[0], forward_one_block, zero_total)
    waveform = matmul_high(inverse, total)
    spill = from_behind(waveform[half:].astype(jnp.bfloat16), "seq", 1).astype(jnp.float32)
    conv = waveform[:half] + spill
    resid = stream_in.astype(jnp.float32) + outer * conv
    scaled = cotangent.astype(jnp.float32) * norm_gain
    square_sum, proj_sum = lax.psum(
        (
            jnp.sum(resid * resid, axis=1, keepdims=True),
            jnp.sum(scaled * resid, axis=1, keepdims=True),
        ),
        "chan",
    )
    total_width = width * lax.axis_size("chan")
    inv_rms = lax.rsqrt(square_sum / total_width + EPSILON)
    normed = (resid * inv_rms * norm_gain).astype(jnp.bfloat16)
    grad_resid = inv_rms * (scaled - resid * inv_rms * inv_rms * (proj_sum / total_width))
    outer_grad = (grad_resid * conv).astype(jnp.bfloat16)
    dconv = grad_resid * outer
    following = from_behind(shortened(dconv), "seq", -1).astype(dconv.dtype)
    back_spec = matmul_high(forward, jnp.concatenate([dconv, following], axis=0)).astype(
        jnp.bfloat16
    )
    backward_piece = lax.all_gather(back_spec[None], "seq", axis=0, tiled=True)

    def backward_one_block(offset, inner_total):
        lag = offset - token_position
        taps = lax.dynamic_index_in_dim(filt_spec, jnp.clip(lag, 0, devices - 1), 0, keepdims=False)
        block = lax.dynamic_index_in_dim(backward_piece, offset, 0, keepdims=False)
        term = spectral_product(block.astype(jnp.float32), taps.astype(jnp.float32), True)
        return inner_total + jnp.where(lag >= 0, term, 0.0)

    back_total = lax.fori_loop(
        0, backward_piece.shape[0], backward_one_block, jnp.zeros((2 * half, width), jnp.float32)
    )
    dmixed = matmul_high(inverse[:half], back_total)
    inner_grad = (dmixed * value_rows).astype(jnp.bfloat16)
    value_grad = (dmixed * inner).astype(jnp.bfloat16)
    return (normed, grad_resid.astype(jnp.bfloat16), outer_grad, inner_grad, value_grad)


def solution(mesh):
    placed = (
        P("seq", "chan"),
        P("seq", "chan"),
        P("seq", "chan"),
        P("seq", "chan"),
        P("seq", "chan"),
        P("chan"),
        P("seq", "chan"),
    )
    return jax.shard_map(
        body,
        mesh=mesh,
        in_specs=placed,
        out_specs=(
            P("seq", "chan"),
            P("seq", "chan"),
            P("seq", "chan"),
            P("seq", "chan"),
            P("seq", "chan"),
        ),
        check_vma=False,
    )
```

profile of v0, /device:TPU:4, one launch (start us, length us, event | category | flops | bytes accessed | tf_op | source)
XLA Modules:
  0.0 370.6 jit_solution(12434627319497629787)
XLA Ops:
  7.3 2.7 select_multiply_fusion
  11.0 1.9 convolution_convert_fusion.2
  13.0 77.7 %all-gather.9.cloned.1.call-done = bf16[4096,256]{1,0:T(8,128)(2,1)} async-done(((bf16[256,256]{1,0:T(8,128)(2,1)}), bf16[4096,256]{1,0:T(8,128)(2,1)}) %all-gather.9.cloned.1.call-update) | async-done | bytes 2097168 | tf_op jit(solution)/shard_map/all_gather | solution.py:80
  90.7 76.4 %all-gather.7.cloned.1.call-done = bf16[4096,256]{1,0:T(8,128)(2,1)} async-done(((bf16[256,256]{1,0:T(8,128)(2,1)}), bf16[4096,256]{1,0:T(8,128)(2,1)}) %all-gather.7.cloned.1.call-update) | async-done | bytes 2097168 | tf_op jit(solution)/shard_map/all_gather | solution.py:82
  167.0 19.8 %while.28 = (s32[]{:T(128)}, f32[256,256]{1,0:T(8,128)S(1)}, s32[]{:T(128)}, bf16[16,256,256]{2,1,0:T(8,128)(2,1)}, bf16[16,256,256]{2,1,0:T(8,128)(2,1)}, /*index=5*/s32[]{:T(128)}, s32[]{:T(128)}, s32[]{:T(128)}) while((s32[]{:T(128)}, f32[256,256]{1,0:T(8,128)S(1)}, s32[]{:T(128)}, bf16[16,256,256]{2,1,0:T(8,128)(2,1)}, ...), condition=%wide.region_1.2_spmd.clone, body=%wide.region_0.1_spmd.clone.sunk | while | flops 655495 | bytes 2359701 | solution.py:91
  168.3 1.0 dynamic-slice_convert_fusion.6
  169.5 1.0 dynamic-slice_convert_fusion.6
  170.7 1.0 dynamic-slice_convert_fusion.6
  172.0 1.0 dynamic-slice_convert_fusion.6
  173.2 1.0 dynamic-slice_convert_fusion.6
  174.5 1.0 dynamic-slice_convert_fusion.6
  175.7 1.0 dynamic-slice_convert_fusion.6
  176.9 1.0 dynamic-slice_convert_fusion.6
  178.2 1.0 dynamic-slice_convert_fusion.6
  179.4 1.0 dynamic-slice_convert_fusion.6
  180.7 1.0 dynamic-slice_convert_fusion.6
  181.9 1.0 dynamic-slice_convert_fusion.6
  183.1 1.0 dynamic-slice_convert_fusion.6
  184.4 1.0 dynamic-slice_convert_fusion.6
  185.6 1.0 dynamic-slice_convert_fusion.6
  186.9 2.2 fusion.23
  189.1 1.5 collective-permute-start
  191.0 1.5 collective-permute-done
  192.6 60.3 %all-reduce = (f32[128,1]{0,1:T(1,128)S(1)}, f32[128,1]{0,1:T(1,128)S(1)}) all-reduce(f32[128,1]{0,1:T(1,128)S(1)} %bitcast.65, f32[128,1]{0,1:T(1,128)S(1)} %bitcast.64), channel_id=1, replica_groups=mesh['seq'=16,'chan'=32] {'chan'}, use_global_device_ids=true, to_apply=%region_3.4 | all-reduce | flops 256 | bytes 2048 | tf_op jit(solution)/shard_map/psum | solution.py:97
  253.1 1.3 collective-permute-start.1
  254.4 5.6 %collective-permute-done.1 = bf16[128,256]{0,1:T(8,128)(2,1)S(1)} collective-permute-done((bf16[128,256]{0,1:T(8,128)(2,1)S(1)}, bf16[128,256]{0,1:T(8,128)(2,1)S(1)}, u32[]{:S(2)}, u32[]{:S(2)}) %collective-permute-start.1) | collective-permute-done | bytes 65568 | tf_op jit(solution)/shard_map/ppermute | solution.py:15
  260.0 2.2 convolution_convert_fusion
  264.5 78.4 %all-gather.11.cloned.1.call-done = bf16[4096,256]{1,0:T(8,128)(2,1)} async-done(((bf16[256,256]{1,0:T(8,128)(2,1)}), bf16[4096,256]{1,0:T(8,128)(2,1)}) %all-gather.11.cloned.1.call-update) | async-done | bytes 2097168 | tf_op jit(solution)/shard_map/all_gather | solution.py:114
  343.0 20.1 %while.29 = (s32[]{:T(128)}, f32[256,256]{1,0:T(8,128)S(1)}, s32[]{:T(128)}, bf16[16,256,256]{2,1,0:T(8,128)(2,1)}, bf16[16,256,256]{2,1,0:T(8,128)(2,1)}, /*index=5*/s32[]{:T(128)}, s32[]{:T(128)}, s32[]{:T(128)}) while((s32[]{:T(128)}, f32[256,256]{1,0:T(8,128)S(1)}, s32[]{:T(128)}, bf16[16,256,256]{2,1,0:T(8,128)(2,1)}, ...), condition=%wide.region_7.8_spmd.clone, body=%wide.region_6.7_spmd.clone.sunk | while | flops 753799 | bytes 2359701 | solution.py:123
  343.0 1.0 dynamic-slice_convert_fusion.7
  350.5 1.0 dynamic-slice_convert_fusion.7
  353.0 1.0 dynamic-slice_convert_fusion.7
  (151 shorter events, 24.9 us)
Async XLA Ops:
  7.2 2.8 copy-start
  7.2 83.5 %all-gather.9.cloned.1.call-start = ((), (), s32[]{:S(2)}) async-start(), calls=%async_computation.1 | async-start | bytes 2228224 | tf_op jit(solution)/shard_map/all_gather | solution.py:80
  10.9 156.1 %all-gather.7.cloned.1.call-start = ((), (), s32[]{:S(2)}) async-start(), calls=%async_computation | async-start | bytes 2228224 | tf_op jit(solution)/shard_map/all_gather | solution.py:82
  12.9 330.1 %all-gather.11.cloned.1.call-start = ((), (), s32[]{:S(2)}) async-start(), calls=%async_computation.2 | async-start | bytes 2228224 | tf_op jit(solution)/shard_map/all_gather | solution.py:114
  186.8 3.8 %copy-start.3 = (bf16[128,256]{1,0:T(8,128)(2,1)S(1)}, bf16[128,256]{1,0:T(8,128)(2,1)}, u32[]{:S(2)}) copy-start(bf16[128,256]{1,0:T(8,128)(2,1)} %param.12) | copy-start | bytes 196612
  186.8 3.9 %copy-start.4 = (bf16[128,256]{1,0:T(8,128)(2,1)S(1)}, bf16[128,256]{1,0:T(8,128)(2,1)}, u32[]{:S(2)}) copy-start(bf16[128,256]{1,0:T(8,128)(2,1)} %param.17) | copy-start | bytes 196612
  186.9 4.0 %copy-start.5 = (bf16[128,256]{1,0:T(8,128)(2,1)S(1)}, bf16[128,256]{1,0:T(8,128)(2,1)}, u32[]{:S(2)}) copy-start(bf16[128,256]{1,0:T(8,128)(2,1)} %param.11) | copy-start | bytes 196612
  186.9 5.6 %copy-start.6 = (f32[256]{0:T(256)S(1)}, f32[256]{0:T(256)}, u32[]{:S(2)}) copy-start(f32[256]{0:T(256)} %param.16) | copy-start | bytes 3076
  189.1 3.4 collective-permute-start
  253.1 6.9 %collective-permute-start.1 = (bf16[128,256]{0,1:T(8,128)(2,1)S(1)}, bf16[128,256]{0,1:T(8,128)(2,1)S(1)}, u32[]{:S(2)}, u32[]{:S(2)}) collective-permute-start(bf16[128,256]{0,1:T(8,128)(2,1)S(1)} %get-tuple-element.260), channel_id=1, source_target_pairs={{32,0},{64,32},{96,64},{128,96},{160,128},{192,160},{224,192},{256... | collective-permute-start | bytes 196616 | tf_op jit(solution)/shard_map/ppermute | solution.py:15
  343.0 20.1 %copy-start.1 = (bf16[128,256]{1,0:T(8,128)(2,1)S(1)}, bf16[128,256]{1,0:T(8,128)(2,1)}, u32[]{:S(2)}) copy-start(bf16[128,256]{1,0:T(8,128)(2,1)} %param.14) | copy-start | bytes 196612
  343.0 20.1 %copy-start.2 = (bf16[128,256]{1,0:T(8,128)(2,1)S(1)}, bf16[128,256]{1,0:T(8,128)(2,1)}, u32[]{:S(2)}) copy-start(bf16[128,256]{1,0:T(8,128)(2,1)} %param.13) | copy-start | bytes 196612
Sparse Core Ops, SparseCore 0:
  11.0 79.5 all-gather.8
  92.8 74.2 all-gather.6
  262.4 80.5 all-gather.10
where the time goes:
time: 371 us
  waiting for transfers between devices  240 us (65%)
  blocking collectives  60.3 us (16%)
  other arithmetic  41.2 us (11%)
  between operations  14 us (4%)
  matrix products  8.16 us (2%)
    all_gather x1, waiting for transfers between devices, body(): backward_piece = lax.all_gather(back_spec[None], 'seq', axis=0, tiled=True)  78.4 us
    all_gather x1, waiting for transfers between devices, body(): filt_spec = lax.all_gather(own_spec[None], 'seq', axis=0, tiled=True)  77.7 us
    all_gather x1, waiting for transfers between devices, body(): piece = lax.all_gather(data_spec[None], 'seq', axis=0, tiled=True)  76.4 us
    psum x1, blocking collectives, body(): lax.psum((jnp.sum(resid * resid, axis=1, keepdims=True), jnp.sum(scaled *...  60.3 us
    convert_element_type x16, other arithmetic, backward_one_block(): taps.astype(jnp.float32)  16.2 us
    convert_element_type x16, other arithmetic, forward_one_block(): taps.astype(jnp.float32)  16.2 us
    dot_general x5, matrix products, matmul_high(): jnp.dot(left, right, precision=HIGHEST_MODE, preferred_element_type=jnp.f...  8.16 us
  transfers between devices with their start and end apart: 5, of which 5 were waited for; matrix products, arithmetic and copies ran while one was open for 1% of the time, Pallas kernels for 0%

commit v1 on v0

v1 whole, which is shorter than its diff:
```python
import math

import numpy as np

import jax
import jax.numpy as jnp
from jax import lax
from jax.sharding import PartitionSpec as P

EPSILON = 1e-06
HIGHEST_MODE = lax.Precision.HIGHEST


def dft_tables(half):
    length = 2 * half
    rows = np.arange(length)[:, None]
    cols = np.arange(length)[None, :]
    step = math.pi / half
    phase = (rows % half * cols % length).astype(np.float64) * step
    nyquist = (half * cols % length).astype(np.float64) * step
    forward = np.where(
        rows < half, np.cos(phase), np.where(rows == half, np.cos(nyquist), -np.sin(phase))
    )
    phase_back = (cols % half * rows % length).astype(np.float64) * step
    nyquist_back = (half * rows % length).astype(np.float64) * step
    weight = np.where(cols == 0, 1.0, 2.0)
    inverse = np.where(
        cols < half,
        weight * np.cos(phase_back),
        np.where(cols == half, np.cos(nyquist_back), -2.0 * np.sin(phase_back)),
    )
    return forward.astype(np.float32), (inverse / length).astype(np.float32)


def spectral_product(left, right, conjugate):
    half = left.shape[-1] // 2
    left_real, left_imag = (left[..., :half], left[..., half:])
    right_real, right_imag = (right[..., :half], right[..., half:])
    first_bin = lax.broadcasted_iota(jnp.int32, (1,) * (left.ndim - 1) + (half,), left.ndim - 1) == 0
    if conjugate:
        right_eff = jnp.where(first_bin, right_imag, -right_imag)
    else:
        right_eff = right_imag
    real_out = left_real * right_real - jnp.where(first_bin, 0.0, left_imag * right_eff)
    imag_out = jnp.where(
        first_bin, left_imag * right_imag, left_real * right_eff + left_imag * right_real
    )
    return jnp.concatenate([real_out, imag_out], axis=-1)


def rows_times(left, table):
    return lax.dot_general(
        left, table, (((left.ndim - 1,), (1,)), ((), ())),
        precision=HIGHEST_MODE, preferred_element_type=jnp.float32,
    )


def to_channels(x, parts):
    tok, width = x.shape[-2], x.shape[-1]
    lead = x.shape[:-2]
    xt = jnp.swapaxes(x, -1, -2).reshape(lead + (parts, width // parts, tok))
    xt = jnp.moveaxis(xt, len(lead), 0)
    return lax.all_to_all(xt, "seq", 0, 0)


def from_channels(xc):
    back = lax.all_to_all(xc, "seq", 0, 0)
    back = jnp.moveaxis(back, 0, -3)
    shape = back.shape
    back = back.reshape(shape[:-3] + (shape[-3] * shape[-2], shape[-1]))
    return jnp.swapaxes(back, -1, -2)


def body(stream_in, outer_gate, inner_gate, values, long_filter, norm_gain, cotangent):
    half = stream_in.shape[0]
    width = stream_in.shape[1]
    parts = lax.axis_size("seq")
    forward_np, inverse_np = dft_tables(half)
    forward = jnp.asarray(forward_np)
    forward_half = jnp.asarray(forward_np[:, :half])
    inverse = jnp.asarray(inverse_np)
    inverse_half = jnp.asarray(inverse_np[:half])

    stacked = jnp.stack([inner_gate, values, long_filter], axis=0)
    chan_in = to_channels(stacked, parts)
    inner_c = chan_in[:, 0].astype(jnp.float32)
    values_c = chan_in[:, 1].astype(jnp.float32)
    filt_c = chan_in[:, 2].astype(jnp.float32)
    blocks = chan_in.shape[0]

    mixed_c = inner_c * values_c
    data_spec = rows_times(mixed_c, forward_half)
    filt_spec = rows_times(filt_c, forward_half)

    total = spectral_product(data_spec, filt_spec[0][None], False)
    for lag in range(1, blocks):
        shifted = jnp.concatenate(
            [jnp.zeros((lag,) + data_spec.shape[1:], jnp.float32), data_spec[: blocks - lag]], axis=0
        )
        total = total + spectral_product(shifted, filt_spec[lag][None], False)
    waveform = rows_times(total, inverse)
    spill = jnp.concatenate(
        [jnp.zeros((1,) + waveform.shape[1:2] + (half,), jnp.float32), waveform[:-1, :, half:]], axis=0
    )
    conv_c = waveform[..., :half] + spill
    conv = from_channels(conv_c)

    outer = outer_gate.astype(jnp.float32)
    resid = stream_in.astype(jnp.float32) + outer * conv
    scaled = cotangent.astype(jnp.float32) * norm_gain
    square_sum, proj_sum = lax.psum(
        (
            jnp.sum(resid * resid, axis=1, keepdims=True),
            jnp.sum(scaled * resid, axis=1, keepdims=True),
        ),
        "chan",
    )
    total_width = width * lax.axis_size("chan")
    inv_rms = lax.rsqrt(square_sum / total_width + EPSILON)
    normed = (resid * inv_rms * norm_gain).astype(jnp.bfloat16)
    grad_resid = inv_rms * (scaled - resid * inv_rms * inv_rms * (proj_sum / total_width))
    outer_grad = (grad_resid * conv).astype(jnp.bfloat16)
    dconv = grad_resid * outer

    dconv_c = to_channels(dconv, parts)
    following = jnp.concatenate([dconv_c[1:], jnp.zeros_like(dconv_c[:1])], axis=0)
    back_spec = rows_times(jnp.concatenate([dconv_c, following], axis=-1), forward)
    back_total = spectral_product(back_spec, filt_spec[0][None], True)
    for lag in range(1, blocks):
        shifted = jnp.concatenate(
            [back_spec[lag:], jnp.zeros((lag,) + back_spec.shape[1:], jnp.float32)], axis=0
        )
        back_total = back_total + spectral_product(shifted, filt_spec[lag][None], True)
    dmixed_c = rows_times(back_total, inverse_half)
    grads_c = jnp.stack(
        [(dmixed_c * values_c).astype(jnp.bfloat16), (dmixed_c * inner_c).astype(jnp.bfloat16)],
        axis=1,
    )
    grads = from_channels(grads_c)
    return (normed, grad_resid.astype(jnp.bfloat16), outer_grad, grads[0], grads[1])


def solution(mesh):
    placed = (
        P("seq", "chan"),
        P("seq", "chan"),
        P("seq", "chan"),
        P("seq", "chan"),
        P("seq", "chan"),
        P("chan"),
        P("seq", "chan"),
    )
    return jax.shard_map(
        body,
        mesh=mesh,
        in_specs=placed,
        out_specs=(
            P("seq", "chan"),
            P("seq", "chan"),
            P("seq", "chan"),
            P("seq", "chan"),
            P("seq", "chan"),
        ),
        check_vma=False,
    )
```

time: 371 us -> 151 us (0.41)
  the two profiles are of different devices: /device:TPU:4 before, /device:TPU:2 now
where the time goes in v1:
time: 151 us
  blocking collectives  110 us (73%)
  local copies, waits for them, and re-layouts  16.2 us (11%)
  starting transfers between devices  9.32 us (6%)
  waiting for transfers between devices  9.16 us (6%)
  other arithmetic  3 us (2%)
  matrix products  2.1 us (1%)
    psum x1, blocking collectives, body(): lax.psum((jnp.sum(resid * resid, axis=1, keepdims=True), jnp.sum(scaled *...  72.4 us
    all_to_all x2, blocking collectives, from_channels(): back = lax.all_to_all(xc, 'seq', 0, 0)  24.6 us
    all_to_all x1, blocking collectives, to_channels(): return lax.all_to_all(xt, 'seq', 0, 0)  12.8 us
    all_to_all x1, starting transfers between devices, to_channels(): return lax.all_to_all(xt, 'seq', 0, 0)  9.32 us
    all_to_all x1, waiting for transfers between devices, to_channels(): return lax.all_to_all(xt, 'seq', 0, 0)  9.16 us
    unnamed x31, local copies, waits for them, and re-layouts  8.14 us
    slice x29, local copies, waits for them, and re-layouts, body(): back_spec[lag:]  3.84 us
    slice x29, local copies, waits for them, and re-layouts, body(): data_spec[:blocks - lag]  3.21 us
  transfers between devices with their start and end apart: 1, of which 1 were waited for; matrix products, arithmetic and copies ran while one was open for 0% of the time, Pallas kernels for 0%

profile of v1, /device:TPU:2, one launch (start us, length us, event | category | flops | bytes accessed | tf_op | source)
XLA Modules:
  0.0 150.6 jit_solution(8064387664580730223)
XLA Ops:
  0.6 1.0 copy.26
  1.8 0.7 copy-done.11
  2.6 0.7 copy.29
  3.3 9.3 %all-to-all-start = ((bf16[16,3,16,128]{3,2,1,0:T(8,128)(2,1)}), bf16[16,3,16,128]{3,2,1,0:T(8,128)(2,1)S(1)}, u32[]{:S(2)}, u32[]{:S(2)}) async-start(bf16[16,3,16,128]{3,2,1,0:T(8,128)(2,1)} %copy.29), calls=%async_computation | async-start | bytes 393216 | tf_op jit(solution)/shard_map/all_to_all | solution.py:63
  12.7 9.2 %all-to-all-done = bf16[16,3,16,128]{3,2,1,0:T(8,128)(2,1)S(1)} async-done(((bf16[16,3,16,128]{3,2,1,0:T(8,128)(2,1)}), bf16[16,3,16,128]{3,2,1,0:T(8,128)(2,1)S(1)}, u32[]{:S(2)}, u32[]{:S(2)}) %all-to-all-start) | async-done | bytes 196640 | tf_op jit(solution)/shard_map/all_to_all | solution.py:63
  21.8 0.4 fusion.38
  22.2 0.7 copy-done.1
  22.9 0.3 fusion.45
  23.3 0.9 copy-done.2
  24.4 0.6 slice-done.14
  25.0 0.3 slice-done.25
  25.6 0.6 slice-done.15
  26.8 0.7 slice-done.16
  27.9 0.8 copy-done.5
  28.7 0.6 fusion.31
  29.3 12.3 %all_to_all.20 = f32[16,16,128]{2,1,0:T(8,128)S(1)} all-to-all(f32[16,16,128]{2,1,0:T(8,128)S(1)} %slice_add_fusion), channel_id=1, replica_groups=mesh['seq'=16,'chan'=32] {'seq'}, dimensions={0} | all-to-all | bytes 262144 | tf_op jit(solution)/shard_map/all_to_all | solution.py:67
  41.7 0.7 copy-done.6
  42.6 72.4 %all-reduce.32 = (f32[128,1]{0,1:T(1,128)S(1)}, f32[128,1]{0,1:T(1,128)S(1)}) all-reduce(f32[128,1]{0,1:T(1,128)S(1)} %bitcast.175, f32[128,1]{0,1:T(1,128)S(1)} %bitcast.174), channel_id=1, replica_groups=mesh['seq'=16,'chan'=32] {'chan'}, use_global_device_ids=true, to_apply=%region_1.2 | all-reduce | flops 256 | bytes 2048 | tf_op jit(solution)/shard_map/psum | solution.py:111
  115.0 0.8 fusion.36
  115.9 12.8 %all_to_all.21 = f32[16,16,128]{2,1,0:T(8,128)S(1)} all-to-all(f32[16,16,128]{2,1,0:T(8,128)S(1)} %bitcast.170), channel_id=1, replica_groups=mesh['seq'=16,'chan'=32] {'seq'}, dimensions={0} | all-to-all | bytes 262144 | tf_op jit(solution)/shard_map/all_to_all | solution.py:63
  128.8 0.4 fusion
  129.2 0.7 copy-done
  130.0 0.9 slice-done.13
  130.9 1.2 select_subtract_fusion
  132.3 0.7 slice-done.2
  133.3 0.7 slice-done.3
  134.4 0.8 slice-done.4
  135.4 0.8 copy-done.8
  136.2 0.5 fusion.44
  136.8 12.3 %all_to_all.22 = bf16[16,2,16,128]{3,2,1,0:T(8,128)(2,1)S(1)} all-to-all(bf16[16,2,16,128]{3,2,1,0:T(8,128)(2,1)S(1)} %copy.35), channel_id=1, replica_groups=mesh['seq'=16,'chan'=32] {'seq'}, dimensions={0} | all-to-all | bytes 262144 | tf_op jit(solution)/shard_map/all_to_all | solution.py:67
  149.2 0.7 copy.38
  149.9 0.7 copy.37
  (96 shorter events, 3.3 us)
Async XLA Ops:
  0.6 1.0 copy-start.10
  3.3 18.5 %copy-start.3 = (f32[256,128,1]{1,0,2:T(8,128)S(1)}, f32[256,128,1]{1,0,2:T(8,128)}, u32[]{:S(2)}) copy-start(f32[256,128,1]{1,0,2:T(8,128)} %constant.102) | copy-start | bytes 393220
  3.3 18.5 %all-to-all-start = ((bf16[16,3,16,128]{3,2,1,0:T(8,128)(2,1)}), bf16[16,3,16,128]{3,2,1,0:T(8,128)(2,1)S(1)}, u32[]{:S(2)}, u32[]{:S(2)}) async-start(bf16[16,3,16,128]{3,2,1,0:T(8,128)(2,1)} %copy.29), calls=%async_computation | async-start | bytes 393216 | tf_op jit(solution)/shard_map/all_to_all | solution.py:63
  23.2 1.0 copy-start.2
  23.3 0.9 slice-start.17
  23.3 1.0 slice-start.18
  24.3 1.0 slice-start.25
  24.3 1.1 slice-start.26
  24.3 1.2 slice-start.27
  25.5 1.0 slice-start.22
  25.5 1.1 slice-start.23
  25.5 1.1 slice-start.24
  26.7 1.0 slice-start.19
  26.7 1.1 slice-start.20
  26.7 1.1 slice-start.21
  27.8 0.9 copy-start.5
  41.6 0.9 copy-start.9
  41.6 0.9 copy-start.12
  115.9 12.9 %copy-start.4 = (f32[256,256,1]{1,0,2:T(8,128)S(1)}, f32[256,256,1]{1,0,2:T(8,128)}, u32[]{:S(2)}) copy-start(f32[256,256,1]{1,0,2:T(8,128)} %constant.104) | copy-start | bytes 786436
  129.9 0.9 slice-start.13
  129.9 0.9 slice-start
  130.9 1.2 slice-start.1
  130.9 1.2 slice-start.11
  130.9 1.2 slice-start.12
  132.1 1.0 slice-start.9
  132.2 1.1 slice-start.10
  133.2 1.0 slice-start.7
  133.2 1.1 slice-start.8
  134.3 0.9 slice-start.4
  134.3 1.0 slice-start.5
  134.3 1.0 slice-start.6
  135.3 0.9 copy-start.8
  (10 other events, 7.9 us)

commit v2 on v1

--- a/solution.py
+++ b/solution.py
@@ -71,6 +71,12 @@
     return jnp.swapaxes(back, -1, -2)
 
 
+def chan_sum(partial):
+    count = lax.axis_size("chan")
+    spread = jnp.broadcast_to(partial[None], (count,) + partial.shape)
+    return jnp.sum(lax.all_to_all(spread, "chan", 0, 0), axis=0)
+
+
 def body(stream_in, outer_gate, inner_gate, values, long_filter, norm_gain, cotangent):
     half = stream_in.shape[0]
     width = stream_in.shape[1]
@@ -108,13 +114,16 @@
     outer = outer_gate.astype(jnp.float32)
     resid = stream_in.astype(jnp.float32) + outer * conv
     scaled = cotangent.astype(jnp.float32) * norm_gain
-    square_sum, proj_sum = lax.psum(
-        (
-            jnp.sum(resid * resid, axis=1, keepdims=True),
-            jnp.sum(scaled * resid, axis=1, keepdims=True),
-        ),
-        "chan",
+    sums = chan_sum(
+        jnp.concatenate(
+            [
+                jnp.sum(resid * resid, axis=1, keepdims=True),
+                jnp.sum(scaled * resid, axis=1, keepdims=True),
+            ],
+            axis=1,
+        )
     )
+    square_sum, proj_sum = sums[:, 0:1], sums[:, 1:2]
     total_width = width * lax.axis_size("chan")
     inv_rms = lax.rsqrt(square_sum / total_width + EPSILON)
     normed = (resid * inv_rms * norm_gain).astype(jnp.bfloat16)

time: 151 us -> 101 us (0.67)
  blocking collectives: 110 us -> 59.9 us
    psum x1 -> x0, blocking collectives: 72.4 us -> none  [body(): lax.psum((jnp.sum(resid * resid, axis=1, keepdims=True), jnp.sum(scaled *...]
    all_to_all x0 -> x1, blocking collectives: none -> 21.7 us  [chan_sum(): return jnp.sum(lax.all_to_all(spread, 'chan', 0, 0), axis=0)]
where the time goes in v2:
time: 101 us
  blocking collectives  59.9 us (59%)
  local copies, waits for them, and re-layouts  16.2 us (16%)
  starting transfers between devices  9.32 us (9%)
  waiting for transfers between devices  9.16 us (9%)
  other arithmetic  3.05 us (3%)
  matrix products  2.1 us (2%)
  between operations  1.05 us (1%)
    all_to_all x2, blocking collectives, from_channels(): back = lax.all_to_all(xc, 'seq', 0, 0)  24.6 us
    all_to_all x1, blocking collectives, chan_sum(): return jnp.sum(lax.all_to_all(spread, 'chan', 0, 0), axis=0)  21.7 us
    all_to_all x1, blocking collectives, to_channels(): return lax.all_to_all(xt, 'seq', 0, 0)  13.6 us
    all_to_all x1, starting transfers between devices, to_channels(): return lax.all_to_all(xt, 'seq', 0, 0)  9.32 us
    all_to_all x1, waiting for transfers between devices, to_channels(): return lax.all_to_all(xt, 'seq', 0, 0)  9.16 us
    unnamed x31, local copies, waits for them, and re-layouts  8.16 us
    slice x29, local copies, waits for them, and re-layouts, body(): back_spec[lag:]  3.84 us
    slice x29, local copies, waits for them, and re-layouts, body(): data_spec[:blocks - lag]  3.17 us
  transfers between devices with their start and end apart: 1, of which 1 were waited for; matrix products, arithmetic and copies ran while one was open for 0% of the time, Pallas kernels for 0%

profile of v2, /device:TPU:2, one launch (start us, length us, event | category | flops | bytes accessed | tf_op | source)
XLA Modules:
  0.0 100.7 jit_solution(6275891388442827156)
XLA Ops:
  0.6 1.0 copy.27
  1.8 0.7 copy-done.11
  2.6 0.7 copy.30
  3.3 9.3 %all-to-all-start = ((bf16[16,3,16,128]{3,2,1,0:T(8,128)(2,1)}), bf16[16,3,16,128]{3,2,1,0:T(8,128)(2,1)S(1)}, u32[]{:S(2)}, u32[]{:S(2)}) async-start(bf16[16,3,16,128]{3,2,1,0:T(8,128)(2,1)} %copy.30), calls=%async_computation | async-start | bytes 393216 | tf_op jit(solution)/shard_map/all_to_all | solution.py:63
  12.7 9.2 %all-to-all-done = bf16[16,3,16,128]{3,2,1,0:T(8,128)(2,1)S(1)} async-done(((bf16[16,3,16,128]{3,2,1,0:T(8,128)(2,1)}), bf16[16,3,16,128]{3,2,1,0:T(8,128)(2,1)S(1)}, u32[]{:S(2)}, u32[]{:S(2)}) %all-to-all-start) | async-done | bytes 196640 | tf_op jit(solution)/shard_map/all_to_all | solution.py:63
  21.8 0.4 fusion.38
  22.2 0.7 copy-done.1
  22.9 0.3 fusion.45
  23.3 0.9 copy-done.2
  24.4 0.6 slice-done.14
  25.0 0.3 slice-done.25
  25.6 0.6 slice-done.15
  26.8 0.7 slice-done.16
  27.8 0.8 copy-done.5
  28.7 0.6 fusion.31
  29.3 12.3 %all_to_all.25 = f32[16,16,128]{2,1,0:T(8,128)S(1)} all-to-all(f32[16,16,128]{2,1,0:T(8,128)S(1)} %slice_add_fusion), channel_id=1, replica_groups=mesh['seq'=16,'chan'=32] {'seq'}, dimensions={0} | all-to-all | bytes 262144 | tf_op jit(solution)/shard_map/all_to_all | solution.py:67
  41.7 0.7 copy-done.6
  42.6 21.7 %all_to_all.26 = f32[32,128,2]{1,2,0:T(2,128)S(1)} all-to-all(f32[32,128,2]{1,2,0:T(2,128)S(1)} %broadcast_in_dim.462), channel_id=1, replica_groups=mesh['seq'=16,'chan'=32] {'chan'}, dimensions={0} | all-to-all | bytes 65536 | tf_op jit(solution)/shard_map/all_to_all | solution.py:77
  64.3 0.8 fusion.36
  65.2 13.6 %all_to_all.27 = f32[16,16,128]{2,1,0:T(8,128)S(1)} all-to-all(f32[16,16,128]{2,1,0:T(8,128)S(1)} %bitcast.170), channel_id=1, replica_groups=mesh['seq'=16,'chan'=32] {'seq'}, dimensions={0} | all-to-all | bytes 262144 | tf_op jit(solution)/shard_map/all_to_all | solution.py:63
  78.9 0.4 fusion
  79.3 0.7 copy-done
  80.1 0.9 slice-done.13
  81.0 1.2 %select_subtract_fusion = (f32[16,16,128]{2,1,0:T(8,128)S(1)}, f32[16,16,128]{2,1,0:T(8,128)S(1)}, f32[16,16,128]{2,1,0:T(8,128)S(1)}, f32[16,16,128]{2,1,0:T(8,...) fusion(f32[1,16,256]{2,1,0:T(8,128)S(1)} %slice-done, f32[16,128]{1,0:T(8,128)S(1)} %get-tuple-element.19, ...), kind=kLoop, calls=%fused_computation.115 | loop fusion | flops 884736 | bytes 1384576 | tf_op jit(solution)/shard_map/sub | solution.py:44
  82.4 0.7 slice-done.2
  83.4 0.7 slice-done.3
  84.5 0.8 slice-done.4
  85.5 0.8 copy-done.8
  86.4 0.5 fusion.44
  86.9 12.3 %all_to_all.28 = bf16[16,2,16,128]{3,2,1,0:T(8,128)(2,1)S(1)} all-to-all(bf16[16,2,16,128]{3,2,1,0:T(8,128)(2,1)S(1)} %copy.36), channel_id=1, replica_groups=mesh['seq'=16,'chan'=32] {'seq'}, dimensions={0} | all-to-all | bytes 262144 | tf_op jit(solution)/shard_map/all_to_all | solution.py:67
  99.3 0.7 copy.39
  100.0 0.7 copy.38
  (99 shorter events, 3.4 us)
Async XLA Ops:
  0.6 1.0 copy-start.10
  3.3 18.5 %copy-start.3 = (f32[256,128,1]{1,0,2:T(8,128)S(1)}, f32[256,128,1]{1,0,2:T(8,128)}, u32[]{:S(2)}) copy-start(f32[256,128,1]{1,0,2:T(8,128)} %constant.102) | copy-start | bytes 393220
  3.3 18.5 %all-to-all-start = ((bf16[16,3,16,128]{3,2,1,0:T(8,128)(2,1)}), bf16[16,3,16,128]{3,2,1,0:T(8,128)(2,1)S(1)}, u32[]{:S(2)}, u32[]{:S(2)}) async-start(bf16[16,3,16,128]{3,2,1,0:T(8,128)(2,1)} %copy.30), calls=%async_computation | async-start | bytes 393216 | tf_op jit(solution)/shard_map/all_to_all | solution.py:63
  23.2 1.0 copy-start.2
  23.3 0.9 slice-start.17
  23.3 1.0 slice-start.18
  24.3 1.0 slice-start.25
  24.3 1.1 %slice-start.26 = ((f32[16,16,256]{2,1,0:T(8,128)}), f32[14,16,256]{2,1,0:T(8,128)S(1)}, s32[]{:S(2)}) async-start(f32[16,16,256]{2,1,0:T(8,128)} %copy-done.1), calls=%async_computation.31 | async-start | bytes 458752 | tf_op jit(solution)/shard_map/slice | solution.py:104
  24.3 1.2 %slice-start.27 = ((f32[16,16,256]{2,1,0:T(8,128)}), f32[15,16,256]{2,1,0:T(8,128)S(1)}, s32[]{:S(2)}) async-start(f32[16,16,256]{2,1,0:T(8,128)} %copy-done.1), calls=%async_computation.32 | async-start | bytes 491520 | tf_op jit(solution)/shard_map/slice | solution.py:104
  25.5 1.0 slice-start.22
  25.5 1.1 %slice-start.23 = ((f32[16,16,256]{2,1,0:T(8,128)}), f32[11,16,256]{2,1,0:T(8,128)S(1)}, s32[]{:S(2)}) async-start(f32[16,16,256]{2,1,0:T(8,128)} %copy-done.1), calls=%async_computation.28 | async-start | bytes 360448 | tf_op jit(solution)/shard_map/slice | solution.py:104
  25.5 1.1 %slice-start.24 = ((f32[16,16,256]{2,1,0:T(8,128)}), f32[12,16,256]{2,1,0:T(8,128)S(1)}, s32[]{:S(2)}) async-start(f32[16,16,256]{2,1,0:T(8,128)} %copy-done.1), calls=%async_computation.29 | async-start | bytes 393216 | tf_op jit(solution)/shard_map/slice | solution.py:104
  26.6 1.0 slice-start.19
  26.6 1.1 %slice-start.20 = ((f32[16,16,256]{2,1,0:T(8,128)}), f32[8,16,256]{2,1,0:T(8,128)S(1)}, s32[]{:S(2)}) async-start(f32[16,16,256]{2,1,0:T(8,128)} %copy-done.1), calls=%async_computation.25 | async-start | bytes 262144 | tf_op jit(solution)/shard_map/slice | solution.py:104
  26.6 1.1 %slice-start.21 = ((f32[16,16,256]{2,1,0:T(8,128)}), f32[9,16,256]{2,1,0:T(8,128)S(1)}, s32[]{:S(2)}) async-start(f32[16,16,256]{2,1,0:T(8,128)} %copy-done.1), calls=%async_computation.26 | async-start | bytes 294912 | tf_op jit(solution)/shard_map/slice | solution.py:104
  27.7 0.9 copy-start.5
  41.6 0.9 copy-start.9
  41.6 0.9 copy-start.12
  65.2 13.7 %copy-start.4 = (f32[256,256,1]{1,0,2:T(8,128)S(1)}, f32[256,256,1]{1,0,2:T(8,128)}, u32[]{:S(2)}) copy-start(f32[256,256,1]{1,0,2:T(8,128)} %constant.104) | copy-start | bytes 786436
  80.0 0.9 slice-start.13
  80.0 0.9 slice-start
  81.0 1.2 %slice-start.1 = ((f32[16,16,256]{2,1,0:T(8,128)}), f32[2,16,256]{2,1,0:T(8,128)S(1)}, s32[]{:S(2)}) async-start(f32[16,16,256]{2,1,0:T(8,128)} %copy-done), calls=%async_computation.6 | async-start | bytes 65536 | tf_op jit(solution)/shard_map/slice | solution.py:140
  81.0 1.2 %slice-start.11 = ((f32[16,16,256]{2,1,0:T(8,128)}), f32[13,16,256]{2,1,0:T(8,128)S(1)}, s32[]{:S(2)}) async-start(f32[16,16,256]{2,1,0:T(8,128)} %copy-done), calls=%async_computation.16 | async-start | bytes 425984 | tf_op jit(solution)/shard_map/slice | solution.py:140
  81.0 1.2 %slice-start.12 = ((f32[16,16,256]{2,1,0:T(8,128)}), f32[14,16,256]{2,1,0:T(8,128)S(1)}, s32[]{:S(2)}) async-start(f32[16,16,256]{2,1,0:T(8,128)} %copy-done), calls=%async_computation.17 | async-start | bytes 458752 | tf_op jit(solution)/shard_map/slice | solution.py:140
  82.3 1.0 slice-start.9
  82.3 1.1 %slice-start.10 = ((f32[16,16,256]{2,1,0:T(8,128)}), f32[12,16,256]{2,1,0:T(8,128)S(1)}, s32[]{:S(2)}) async-start(f32[16,16,256]{2,1,0:T(8,128)} %copy-done), calls=%async_computation.15 | async-start | bytes 393216 | tf_op jit(solution)/shard_map/slice | solution.py:140
  83.3 1.0 slice-start.7
  83.3 1.1 %slice-start.8 = ((f32[16,16,256]{2,1,0:T(8,128)}), f32[10,16,256]{2,1,0:T(8,128)S(1)}, s32[]{:S(2)}) async-start(f32[16,16,256]{2,1,0:T(8,128)} %copy-done), calls=%async_computation.13 | async-start | bytes 327680 | tf_op jit(solution)/shard_map/slice | solution.py:140
  84.4 0.9 slice-start.4
  84.4 1.0 slice-start.5
  84.4 1.0 %slice-start.6 = ((f32[16,16,256]{2,1,0:T(8,128)}), f32[8,16,256]{2,1,0:T(8,128)S(1)}, s32[]{:S(2)}) async-start(f32[16,16,256]{2,1,0:T(8,128)} %copy-done), calls=%async_computation.11 | async-start | bytes 262144 | tf_op jit(solution)/shard_map/slice | solution.py:140
  85.5 0.9 copy-start.8
  (10 other events, 7.9 us)

commit v3 on v2

--- a/solution.py
+++ b/solution.py
@@ -109,7 +109,7 @@
         [jnp.zeros((1,) + waveform.shape[1:2] + (half,), jnp.float32), waveform[:-1, :, half:]], axis=0
     )
     conv_c = waveform[..., :half] + spill
-    conv = from_channels(conv_c)
+    conv = from_channels(conv_c.astype(jnp.bfloat16)).astype(jnp.float32)
 
     outer = outer_gate.astype(jnp.float32)
     resid = stream_in.astype(jnp.float32) + outer * conv
@@ -131,7 +131,7 @@
     outer_grad = (grad_resid * conv).astype(jnp.bfloat16)
     dconv = grad_resid * outer
 
-    dconv_c = to_channels(dconv, parts)
+    dconv_c = to_channels(dconv.astype(jnp.bfloat16), parts).astype(jnp.float32)
     following = jnp.concatenate([dconv_c[1:], jnp.zeros_like(dconv_c[:1])], axis=0)
     back_spec = rows_times(jnp.concatenate([dconv_c, following], axis=-1), forward)
     back_total = spectral_product(back_spec, filt_spec[0][None], True)

time: 101 us -> 99.7 us (0.987)
  blocking collectives: 59.9 us -> 58 us
    all_to_all x1, blocking collectives: 13.6 us -> 12.4 us  [to_channels(): return lax.all_to_all(xt, 'seq', 0, 0)]
where the time goes in v3:
time: 99.7 us; the launch traced here: 98.9 us
  blocking collectives  58 us (58%)
  local copies, waits for them, and re-layouts  16.2 us (16%)
  starting transfers between devices  9.32 us (9%)
  waiting for transfers between devices  9.16 us (9%)
  other arithmetic  3.09 us (3%)
  matrix products  2.1 us (2%)
  between operations  1.08 us (1%)
    all_to_all x2, blocking collectives, from_channels(): back = lax.all_to_all(xc, 'seq', 0, 0)  23.9 us
    all_to_all x1, blocking collectives, chan_sum(): return jnp.sum(lax.all_to_all(spread, 'chan', 0, 0), axis=0)  21.7 us
    all_to_all x1, blocking collectives, to_channels(): return lax.all_to_all(xt, 'seq', 0, 0)  12.4 us
    all_to_all x1, starting transfers between devices, to_channels(): return lax.all_to_all(xt, 'seq', 0, 0)  9.32 us
    all_to_all x1, waiting for transfers between devices, to_channels(): return lax.all_to_all(xt, 'seq', 0, 0)  9.16 us
    unnamed x31, local copies, waits for them, and re-layouts  8.14 us
    slice x29, local copies, waits for them, and re-layouts, body(): back_spec[lag:]  3.84 us
    slice x29, local copies, waits for them, and re-layouts, body(): data_spec[:blocks - lag]  3.17 us
  transfers between devices with their start and end apart: 1, of which 1 were waited for; matrix products, arithmetic and copies ran while one was open for 0% of the time, Pallas kernels for 0%

profile of v3, /device:TPU:2, one launch (start us, length us, event | category | flops | bytes accessed | tf_op | source)
XLA Modules:
  0.0 98.9 jit_solution(1972233980148486170)
XLA Ops:
  0.6 1.0 copy.27
  1.8 0.7 copy-done.11
  2.6 0.7 copy.30
  3.3 9.3 %all-to-all-start = ((bf16[16,3,16,128]{3,2,1,0:T(8,128)(2,1)}), bf16[16,3,16,128]{3,2,1,0:T(8,128)(2,1)S(1)}, u32[]{:S(2)}, u32[]{:S(2)}) async-start(bf16[16,3,16,128]{3,2,1,0:T(8,128)(2,1)} %copy.30), calls=%async_computation | async-start | bytes 393216 | tf_op jit(solution)/shard_map/all_to_all | solution.py:63
  12.7 9.2 %all-to-all-done = bf16[16,3,16,128]{3,2,1,0:T(8,128)(2,1)S(1)} async-done(((bf16[16,3,16,128]{3,2,1,0:T(8,128)(2,1)}), bf16[16,3,16,128]{3,2,1,0:T(8,128)(2,1)S(1)}, u32[]{:S(2)}, u32[]{:S(2)}) %all-to-all-start) | async-done | bytes 196640 | tf_op jit(solution)/shard_map/all_to_all | solution.py:63
  21.8 0.4 fusion.38
  22.2 0.7 copy-done.1
  22.9 0.3 fusion.47
  23.3 0.9 copy-done.2
  24.4 0.6 slice-done.14
  25.0 0.3 slice-done.25
  25.6 0.6 slice-done.15
  26.8 0.7 slice-done.16
  27.8 0.8 copy-done.5
  28.7 0.6 fusion.31
  29.3 11.6 %all_to_all.25 = bf16[16,16,128]{2,1,0:T(8,128)(2,1)S(1)} all-to-all(bf16[16,16,128]{2,1,0:T(8,128)(2,1)S(1)} %fusion.42), channel_id=1, replica_groups=mesh['seq'=16,'chan'=32] {'seq'}, dimensions={0} | all-to-all | bytes 131072 | tf_op jit(solution)/shard_map/all_to_all | solution.py:67
  41.1 0.7 copy-done.6
  42.0 21.7 %all_to_all.26 = f32[32,128,2]{1,2,0:T(2,128)S(1)} all-to-all(f32[32,128,2]{1,2,0:T(2,128)S(1)} %broadcast_in_dim.462), channel_id=1, replica_groups=mesh['seq'=16,'chan'=32] {'chan'}, dimensions={0} | all-to-all | bytes 65536 | tf_op jit(solution)/shard_map/all_to_all | solution.py:77
  63.7 0.8 fusion.46
  64.6 12.4 %all_to_all.27 = bf16[16,16,128]{2,1,0:T(8,128)(2,1)S(1)} all-to-all(bf16[16,16,128]{2,1,0:T(8,128)(2,1)S(1)} %bitcast.171), channel_id=1, replica_groups=mesh['seq'=16,'chan'=32] {'seq'}, dimensions={0} | all-to-all | bytes 131072 | tf_op jit(solution)/shard_map/all_to_all | solution.py:63
  77.1 0.4 fusion
  77.5 0.7 copy-done
  78.3 0.9 slice-done.13
  79.2 1.2 %select_subtract_fusion = (f32[16,16,128]{2,1,0:T(8,128)S(1)}, f32[16,16,128]{2,1,0:T(8,128)S(1)}, f32[16,16,128]{2,1,0:T(8,128)S(1)}, f32[16,16,128]{2,1,0:T(8,...) fusion(f32[1,16,256]{2,1,0:T(8,128)S(1)} %slice-done, f32[16,128]{1,0:T(8,128)S(1)} %get-tuple-element.19, ...), kind=kLoop, calls=%fused_computation.116 | loop fusion | flops 884736 | bytes 1384576 | tf_op jit(solution)/shard_map/sub | solution.py:44
  80.6 0.7 slice-done.2
  81.6 0.7 slice-done.3
  82.7 0.8 slice-done.4
  83.7 0.8 copy-done.8
  84.5 0.5 fusion.45
  85.1 12.3 %all_to_all.28 = bf16[16,2,16,128]{3,2,1,0:T(8,128)(2,1)S(1)} all-to-all(bf16[16,2,16,128]{3,2,1,0:T(8,128)(2,1)S(1)} %copy.36), channel_id=1, replica_groups=mesh['seq'=16,'chan'=32] {'seq'}, dimensions={0} | all-to-all | bytes 262144 | tf_op jit(solution)/shard_map/all_to_all | solution.py:67
  97.4 0.7 copy.39
  98.2 0.7 copy.38
  (101 shorter events, 3.4 us)
Async XLA Ops:
  0.6 1.0 %copy-start.10 = (bf16[128,256]{1,0:T(8,128)(2,1)S(1)}, bf16[128,256]{1,0:T(8,128)(2,1)}, u32[]{:S(2)}) copy-start(bf16[128,256]{1,0:T(8,128)(2,1)} %param.14) | copy-start | bytes 196612
  3.3 18.5 %copy-start.3 = (f32[256,128,1]{1,0,2:T(8,128)S(1)}, f32[256,128,1]{1,0,2:T(8,128)}, u32[]{:S(2)}) copy-start(f32[256,128,1]{1,0,2:T(8,128)} %constant.102) | copy-start | bytes 393220
  3.3 18.5 %all-to-all-start = ((bf16[16,3,16,128]{3,2,1,0:T(8,128)(2,1)}), bf16[16,3,16,128]{3,2,1,0:T(8,128)(2,1)S(1)}, u32[]{:S(2)}, u32[]{:S(2)}) async-start(bf16[16,3,16,128]{3,2,1,0:T(8,128)(2,1)} %copy.30), calls=%async_computation | async-start | bytes 393216 | tf_op jit(solution)/shard_map/all_to_all | solution.py:63
  23.2 1.0 copy-start.2
  23.3 0.9 slice-start.17
  23.3 1.0 %slice-start.18 = ((f32[16,16,256]{2,1,0:T(8,128)}), f32[5,16,256]{2,1,0:T(8,128)S(1)}, s32[]{:S(2)}) async-start(f32[16,16,256]{2,1,0:T(8,128)} %copy-done.1), calls=%async_computation.23 | async-start | bytes 163840 | tf_op jit(solution)/shard_map/slice | solution.py:104
  24.3 1.0 %slice-start.25 = ((f32[16,16,256]{2,1,0:T(8,128)}), f32[13,16,256]{2,1,0:T(8,128)S(1)}, s32[]{:S(2)}) async-start(f32[16,16,256]{2,1,0:T(8,128)} %copy-done.1), calls=%async_computation.30 | async-start | bytes 425984 | tf_op jit(solution)/shard_map/slice | solution.py:104
  24.3 1.1 %slice-start.26 = ((f32[16,16,256]{2,1,0:T(8,128)}), f32[14,16,256]{2,1,0:T(8,128)S(1)}, s32[]{:S(2)}) async-start(f32[16,16,256]{2,1,0:T(8,128)} %copy-done.1), calls=%async_computation.31 | async-start | bytes 458752 | tf_op jit(solution)/shard_map/slice | solution.py:104
  24.3 1.2 %slice-start.27 = ((f32[16,16,256]{2,1,0:T(8,128)}), f32[15,16,256]{2,1,0:T(8,128)S(1)}, s32[]{:S(2)}) async-start(f32[16,16,256]{2,1,0:T(8,128)} %copy-done.1), calls=%async_computation.32 | async-start | bytes 491520 | tf_op jit(solution)/shard_map/slice | solution.py:104
  25.5 1.0 %slice-start.22 = ((f32[16,16,256]{2,1,0:T(8,128)}), f32[10,16,256]{2,1,0:T(8,128)S(1)}, s32[]{:S(2)}) async-start(f32[16,16,256]{2,1,0:T(8,128)} %copy-done.1), calls=%async_computation.27 | async-start | bytes 327680 | tf_op jit(solution)/shard_map/slice | solution.py:104
  25.5 1.1 %slice-start.23 = ((f32[16,16,256]{2,1,0:T(8,128)}), f32[11,16,256]{2,1,0:T(8,128)S(1)}, s32[]{:S(2)}) async-start(f32[16,16,256]{2,1,0:T(8,128)} %copy-done.1), calls=%async_computation.28 | async-start | bytes 360448 | tf_op jit(solution)/shard_map/slice | solution.py:104
  25.5 1.1 %slice-start.24 = ((f32[16,16,256]{2,1,0:T(8,128)}), f32[12,16,256]{2,1,0:T(8,128)S(1)}, s32[]{:S(2)}) async-start(f32[16,16,256]{2,1,0:T(8,128)} %copy-done.1), calls=%async_computation.29 | async-start | bytes 393216 | tf_op jit(solution)/shard_map/slice | solution.py:104
  26.6 1.0 slice-start.19
  26.6 1.1 %slice-start.20 = ((f32[16,16,256]{2,1,0:T(8,128)}), f32[8,16,256]{2,1,0:T(8,128)S(1)}, s32[]{:S(2)}) async-start(f32[16,16,256]{2,1,0:T(8,128)} %copy-done.1), calls=%async_computation.25 | async-start | bytes 262144 | tf_op jit(solution)/shard_map/slice | solution.py:104
  26.6 1.1 %slice-start.21 = ((f32[16,16,256]{2,1,0:T(8,128)}), f32[9,16,256]{2,1,0:T(8,128)S(1)}, s32[]{:S(2)}) async-start(f32[16,16,256]{2,1,0:T(8,128)} %copy-done.1), calls=%async_computation.26 | async-start | bytes 294912 | tf_op jit(solution)/shard_map/slice | solution.py:104
  27.7 0.9 copy-start.5
  40.9 0.9 copy-start.9
  40.9 0.9 copy-start.12
  64.6 12.5 %copy-start.4 = (f32[256,256,1]{1,0,2:T(8,128)S(1)}, f32[256,256,1]{1,0,2:T(8,128)}, u32[]{:S(2)}) copy-start(f32[256,256,1]{1,0,2:T(8,128)} %constant.104) | copy-start | bytes 786436
  78.2 0.9 slice-start.13
  78.2 0.9 slice-start
  79.2 1.2 %slice-start.1 = ((f32[16,16,256]{2,1,0:T(8,128)}), f32[2,16,256]{2,1,0:T(8,128)S(1)}, s32[]{:S(2)}) async-start(f32[16,16,256]{2,1,0:T(8,128)} %copy-done), calls=%async_computation.6 | async-start | bytes 65536 | tf_op jit(solution)/shard_map/slice | solution.py:140
  79.2 1.2 %slice-start.11 = ((f32[16,16,256]{2,1,0:T(8,128)}), f32[13,16,256]{2,1,0:T(8,128)S(1)}, s32[]{:S(2)}) async-start(f32[16,16,256]{2,1,0:T(8,128)} %copy-done), calls=%async_computation.16 | async-start | bytes 425984 | tf_op jit(solution)/shard_map/slice | solution.py:140
  79.2 1.2 %slice-start.12 = ((f32[16,16,256]{2,1,0:T(8,128)}), f32[14,16,256]{2,1,0:T(8,128)S(1)}, s32[]{:S(2)}) async-start(f32[16,16,256]{2,1,0:T(8,128)} %copy-done), calls=%async_computation.17 | async-start | bytes 458752 | tf_op jit(solution)/shard_map/slice | solution.py:140
  80.4 1.0 %slice-start.9 = ((f32[16,16,256]{2,1,0:T(8,128)}), f32[11,16,256]{2,1,0:T(8,128)S(1)}, s32[]{:S(2)}) async-start(f32[16,16,256]{2,1,0:T(8,128)} %copy-done), calls=%async_computation.14 | async-start | bytes 360448 | tf_op jit(solution)/shard_map/slice | solution.py:140
  80.4 1.1 %slice-start.10 = ((f32[16,16,256]{2,1,0:T(8,128)}), f32[12,16,256]{2,1,0:T(8,128)S(1)}, s32[]{:S(2)}) async-start(f32[16,16,256]{2,1,0:T(8,128)} %copy-done), calls=%async_computation.15 | async-start | bytes 393216 | tf_op jit(solution)/shard_map/slice | solution.py:140
  81.5 1.0 %slice-start.7 = ((f32[16,16,256]{2,1,0:T(8,128)}), f32[9,16,256]{2,1,0:T(8,128)S(1)}, s32[]{:S(2)}) async-start(f32[16,16,256]{2,1,0:T(8,128)} %copy-done), calls=%async_computation.12 | async-start | bytes 294912 | tf_op jit(solution)/shard_map/slice | solution.py:140
  81.5 1.1 %slice-start.8 = ((f32[16,16,256]{2,1,0:T(8,128)}), f32[10,16,256]{2,1,0:T(8,128)S(1)}, s32[]{:S(2)}) async-start(f32[16,16,256]{2,1,0:T(8,128)} %copy-done), calls=%async_computation.13 | async-start | bytes 327680 | tf_op jit(solution)/shard_map/slice | solution.py:140
  82.6 0.9 slice-start.4
  82.6 1.0 slice-start.5
  82.6 1.0 %slice-start.6 = ((f32[16,16,256]{2,1,0:T(8,128)}), f32[8,16,256]{2,1,0:T(8,128)S(1)}, s32[]{:S(2)}) async-start(f32[16,16,256]{2,1,0:T(8,128)} %copy-done), calls=%async_computation.11 | async-start | bytes 262144 | tf_op jit(solution)/shard_map/slice | solution.py:140
  83.6 0.9 copy-start.8
  (10 other events, 7.9 us)

commit v4 on v3

--- a/solution.py
+++ b/solution.py
@@ -5,6 +5,8 @@
 import jax
 import jax.numpy as jnp
 from jax import lax
+from jax.experimental import pallas as pl
+from jax.experimental.pallas import tpu as pltpu
 from jax.sharding import PartitionSpec as P
 
 EPSILON = 1e-06
@@ -55,6 +57,93 @@
     )
 
 
+def packed_product(left, right, conjugate):
+    half = left.shape[-1] // 2
+    left_real, left_imag = (left[:, :half], left[:, half:])
+    right_real, right_imag = (right[:, :half], right[:, half:])
+    first_bin = lax.broadcasted_iota(jnp.int32, left_real.shape, 1) == 0
+    if conjugate:
+        right_eff = jnp.where(first_bin, right_imag, -right_imag)
+    else:
+        right_eff = right_imag
+    real_out = left_real * right_real - jnp.where(first_bin, 0.0, left_imag * right_eff)
+    imag_out = jnp.where(
+        first_bin, left_imag * right_imag, left_real * right_eff + left_imag * right_real
+    )
+    return real_out, imag_out
+
+
+def kdot(left, right):
+    return jnp.dot(left, right, precision=HIGHEST_MODE, preferred_element_type=jnp.float32)
+
+
+def tiled_rows(part, count):
+    rows, lanes = part.shape
+    return jnp.broadcast_to(part[None], (count, rows, lanes)).reshape(count * rows, lanes)
+
+
+def forward_kernel(x_ref, fwd_ref, inv_ref, conv_ref, filt_ref, acc_ref):
+    blocks, _, chans, tok = x_ref.shape
+    rows = blocks * chans
+    inner = x_ref[:, 0, :, :].astype(jnp.float32).reshape(rows, tok)
+    value_rows = x_ref[:, 1, :, :].astype(jnp.float32).reshape(rows, tok)
+    taps = x_ref[:, 2, :, :].astype(jnp.float32).reshape(rows, tok)
+    table = fwd_ref[...]
+    data_spec = kdot(inner * value_rows, table)
+    filt_spec = kdot(taps, table)
+    filt_ref[...] = filt_spec
+    half = data_spec.shape[1] // 2
+    real0, imag0 = packed_product(data_spec, tiled_rows(filt_spec[0:chans], blocks), False)
+    acc_ref[:, :half] = real0
+    acc_ref[:, half:] = imag0
+    for lag in range(1, blocks):
+        count = blocks - lag
+        real, imag = packed_product(
+            data_spec[: count * chans], tiled_rows(filt_spec[lag * chans : (lag + 1) * chans], count), False
+        )
+        acc_ref[lag * chans :, :half] += real
+        acc_ref[lag * chans :, half:] += imag
+    waveform = kdot(acc_ref[...], inv_ref[...])
+    conv_ref[0:chans, :] = waveform[0:chans, :tok].astype(conv_ref.dtype)
+    conv_ref[chans:, :] = (waveform[chans:, :tok] + waveform[: rows - chans, tok:]).astype(conv_ref.dtype)
+
+
+def backward_kernel(d_ref, filt_ref, x_ref, fwd_ref, inv_ref, out_ref, fol_ref, acc_ref):
+    blocks, _, chans, tok = x_ref.shape
+    rows = blocks * chans
+    dconv = d_ref[...].astype(jnp.float32)
+    fol_ref[: rows - chans, :] = dconv[chans:, :]
+    fol_ref[rows - chans :, :] = jnp.zeros((chans, tok), jnp.float32)
+    back_spec = kdot(dconv, fwd_ref[:tok, :]) + kdot(fol_ref[...], fwd_ref[tok:, :])
+    filt_spec = filt_ref[...]
+    half = back_spec.shape[1] // 2
+    real0, imag0 = packed_product(back_spec, tiled_rows(filt_spec[0:chans], blocks), True)
+    acc_ref[:, :half] = real0
+    acc_ref[:, half:] = imag0
+    for lag in range(1, blocks):
+        count = blocks - lag
+        real, imag = packed_product(
+            back_spec[lag * chans :], tiled_rows(filt_spec[lag * chans : (lag + 1) * chans], count), True
+        )
+        acc_ref[: count * chans, :half] += real
+        acc_ref[: count * chans, half:] += imag
+    dmixed = kdot(acc_ref[...], inv_ref[...]).reshape(blocks, chans, tok)
+    inner = x_ref[:, 0, :, :].astype(jnp.float32)
+    value_rows = x_ref[:, 1, :, :].astype(jnp.float32)
+    out_ref[:, 0, :, :] = (dmixed * value_rows).astype(out_ref.dtype)
+    out_ref[:, 1, :, :] = (dmixed * inner).astype(out_ref.dtype)
+
+
+def vmem_call(kernel, outs, scratch, *args):
+    return pl.pallas_call(
+        kernel,
+        out_shape=outs,
+        in_specs=[pl.BlockSpec(memory_space=pltpu.VMEM) for _ in args],
+        out_specs=tuple(pl.BlockSpec(memory_space=pltpu.VMEM) for _ in outs),
+        scratch_shapes=scratch,
+    )(*args)
+
+
 def to_channels(x, parts):
     tok, width = x.shape[-2], x.shape[-1]
     lead = x.shape[:-2]
@@ -82,34 +171,22 @@
     width = stream_in.shape[1]
     parts = lax.axis_size("seq")
     forward_np, inverse_np = dft_tables(half)
-    forward = jnp.asarray(forward_np)
-    forward_half = jnp.asarray(forward_np[:, :half])
-    inverse = jnp.asarray(inverse_np)
-    inverse_half = jnp.asarray(inverse_np[:half])
 
     stacked = jnp.stack([inner_gate, values, long_filter], axis=0)
     chan_in = to_channels(stacked, parts)
-    inner_c = chan_in[:, 0].astype(jnp.float32)
-    values_c = chan_in[:, 1].astype(jnp.float32)
-    filt_c = chan_in[:, 2].astype(jnp.float32)
-    blocks = chan_in.shape[0]
-
-    mixed_c = inner_c * values_c
-    data_spec = rows_times(mixed_c, forward_half)
-    filt_spec = rows_times(filt_c, forward_half)
-
-    total = spectral_product(data_spec, filt_spec[0][None], False)
-    for lag in range(1, blocks):
-        shifted = jnp.concatenate(
-            [jnp.zeros((lag,) + data_spec.shape[1:], jnp.float32), data_spec[: blocks - lag]], axis=0
-        )
-        total = total + spectral_product(shifted, filt_spec[lag][None], False)
-    waveform = rows_times(total, inverse)
-    spill = jnp.concatenate(
-        [jnp.zeros((1,) + waveform.shape[1:2] + (half,), jnp.float32), waveform[:-1, :, half:]], axis=0
-    )
-    conv_c = waveform[..., :half] + spill
-    conv = from_channels(conv_c.astype(jnp.bfloat16)).astype(jnp.float32)
+    blocks, _, chans, tok = chan_in.shape
+    rows = blocks * chans
+    conv_c, filt_spec = vmem_call(
+        forward_kernel,
+        (
+            jax.ShapeDtypeStruct((rows, tok), jnp.bfloat16),
+            jax.ShapeDtypeStruct((rows, 2 * half), jnp.float32),
+        ),
+        [pltpu.VMEM((rows, 2 * half), jnp.float32)],
+        chan_in, jnp.asarray(forward_np[:, :half].T), jnp.asarray(inverse_np.T),
+    )
+    conv_c = conv_c.reshape(blocks, chans, tok)
+    conv = from_channels(conv_c).astype(jnp.float32)
 
     outer = outer_gate.astype(jnp.float32)
     resid = stream_in.astype(jnp.float32) + outer * conv
@@ -131,19 +208,12 @@
     outer_grad = (grad_resid * conv).astype(jnp.bfloat16)
     dconv = grad_resid * outer
 
-    dconv_c = to_channels(dconv.astype(jnp.bfloat16), parts).astype(jnp.float32)
-    following = jnp.concatenate([dconv_c[1:], jnp.zeros_like(dconv_c[:1])], axis=0)
-    back_spec = rows_times(jnp.concatenate([dconv_c, following], axis=-1), forward)
-    back_total = spectral_product(back_spec, filt_spec[0][None], True)
-    for lag in range(1, blocks):
-        shifted = jnp.concatenate(
-            [back_spec[lag:], jnp.zeros((lag,) + back_spec.shape[1:], jnp.float32)], axis=0
-        )
-        back_total = back_total + spectral_product(shifted, filt_spec[lag][None], True)
-    dmixed_c = rows_times(back_total, inverse_half)
-    grads_c = jnp.stack(
-        [(dmixed_c * values_c).astype(jnp.bfloat16), (dmixed_c * inner_c).astype(jnp.bfloat16)],
-        axis=1,
+    dconv_c = to_channels(dconv.astype(jnp.bfloat16), parts).reshape(rows, tok)
+    (grads_c,) = vmem_call(
+        backward_kernel,
+        (jax.ShapeDtypeStruct((blocks, 2, chans, tok), jnp.bfloat16),),
+        [pltpu.VMEM((rows, tok), jnp.float32), pltpu.VMEM((rows, 2 * half), jnp.float32)],
+        dconv_c, filt_spec, chan_in, jnp.asarray(forward_np.T), jnp.asarray(inverse_np[:half].T),
     )
     grads = from_channels(grads_c)
     return (normed, grad_resid.astype(jnp.bfloat16), outer_grad, grads[0], grads[1])

time: 99.7 us -> 90.6 us (0.909)
  local copies, waits for them, and re-layouts: 16.2 us -> 7.46 us
  Pallas kernels: 0 us -> 6.71 us
  blocking collectives: 58 us -> 53.1 us
  waiting for transfers between devices: 9.16 us -> 12.2 us
  other arithmetic: 3.09 us -> 0.34 us
  matrix products: 2.1 us -> 0 us
    all_to_all x2 -> x0, blocking collectives: 23.9 us -> none  [from_channels(): back = lax.all_to_all(xc, 'seq', 0, 0)]
    all_to_all x1 -> x2, blocking collectives: 12.4 us -> 31.2 us  [to_channels(): return lax.all_to_all(xt, 'seq', 0, 0)]
    slice x60 -> x0, local copies, waits for them, and re-layouts: 7.04 us -> none  [the longest x29 3.84 us: body(): back_spec[lag:]]
    pallas_call x0 -> x2, Pallas kernels: none -> 6.71 us  [vmem_call(): pl.pallas_call(kernel, out_shape=outs, in_specs=[pl.BlockSpec(memory_spac...]
    all_to_all x1 -> x2, waiting for transfers between devices: 9.16 us -> 12.2 us  [from_channels(): back = lax.all_to_all(xc, 'seq', 0, 0)]
    dot_general x5 -> x0, matrix products: 2.1 us -> none  [rows_times(): lax.dot_general(left, table, (((left.ndim - 1,), (1,)), ((), ())), precis...]
    sub x10 -> x0, other arithmetic: 1.98 us -> none  [spectral_product(): left_real * right_real - jnp.where(first_bin, 0.0, left_imag * right_eff)]
    unnamed x31 -> x23, local copies, waits for them, and re-layouts: 8.14 us -> 7.41 us
  transfers between devices with their start and end apart: 1 -> 2, of which waited for: 1 -> 2; matrix products, arithmetic and copies ran while one was open for 0% -> 3% of each run, Pallas kernels for 0% -> 0%
where the time goes in v4:
time: 90.6 us; the launch traced here: 90 us
  blocking collectives  53.1 us (59%)
  waiting for transfers between devices  12.2 us (13%)
  starting transfers between devices  9.38 us (10%)
  local copies, waits for them, and re-layouts  7.46 us (8%)
  Pallas kernels  6.71 us (7%)
    all_to_all x2, blocking collectives, to_channels(): return lax.all_to_all(xt, 'seq', 0, 0)  31.2 us
    all_to_all x1, blocking collectives, chan_sum(): return jnp.sum(lax.all_to_all(spread, 'chan', 0, 0), axis=0)  21.9 us
    all_to_all x2, waiting for transfers between devices, from_channels(): back = lax.all_to_all(xc, 'seq', 0, 0)  12.2 us
    all_to_all x2, starting transfers between devices, from_channels(): back = lax.all_to_all(xc, 'seq', 0, 0)  9.38 us
    unnamed x23, local copies, waits for them, and re-layouts  7.41 us
    pallas_call x2, Pallas kernels, vmem_call(): pl.pallas_call(kernel, out_shape=outs, in_specs=[pl.BlockSpec(memory_spac...  6.71 us
  transfers between devices with their start and end apart: 2, of which 2 were waited for; matrix products, arithmetic and copies ran while one was open for 3% of the time, Pallas kernels for 0%

profile of v4, /device:TPU:2, one launch (start us, length us, event | category | flops | bytes accessed | tf_op | source)
XLA Modules:
  0.0 90.0 jit_solution(7245301300289799352)
XLA Ops:
  0.6 0.0 copy-start
  0.6 1.0 %copy.35 = bf16[128,256]{0,1:T(8,128)(2,1)S(1)} copy(bf16[128,256]{1,0:T(8,128)(2,1)} %param.13) | data formatting | bytes 131072 | tf_op args[2]
  1.6 0.0 copy-done
  1.6 0.0 copy-start.1
  1.6 0.1 copy.36
  1.8 0.7 copy-done.1
  2.5 0.1 copy.37
  2.7 18.3 %all_to_all.25.x_ref = bf16[16,3,16,128]{3,2,1,0:T(8,128)(2,1)} all-to-all(bf16[16,3,16,128]{3,2,1,0:T(8,128)(2,1)S(1)} %bitcast.69), channel_id=1, replica_groups=mesh['seq'=16,'chan'=32] {'seq'}, dimensions={0} | all-to-all | bytes 393216 | tf_op jit(solution)/shard_map/all_to_all | solution.py:152
  20.9 3.3 %shard_map.146 = (bf16[256,128]{1,0:T(8,128)(2,1)}, f32[256,256]{1,0:T(8,128)}) custom-call(bf16[16,3,16,128]{3,2,1,0:T(8,128)(2,1)} %all_to_all.25.x_ref, f32[128,256]{1,0:T(8,128)} %constant.16.clone.fwd_ref, f32[256,256]{1,0:T(8,128)} %constant.17.clone.inv_ref), custom_call_target="tpu_custom_call" | custom-call | tf_op jit(solution)/shard_map/pallas_call | solution.py:138
  24.3 0.0 copy-start.2
  24.3 4.6 %all-to-all-start.1 = ((bf16[16,16,128]{2,1,0:T(8,128)(2,1)}), bf16[16,16,128]{2,1,0:T(8,128)(2,1)S(1)}, u32[]{:S(2)}, u32[]{:S(2)}) async-start(bf16[16,16,128]{2,1,0:T(8,128)(2,1)} %bitcast.77), calls=%async_computation.1 | async-start | bytes 131072 | tf_op jit(solution)/shard_map/all_to_all | solution.py:156
  28.9 0.0 copy-done.2
  28.9 0.0 copy-start.3
  28.9 0.1 copy.33
  29.0 0.7 copy-done.3
  29.7 0.1 copy.34
  29.8 0.7 copy-done.4
  30.6 0.1 copy.39
  30.7 6.0 %all-to-all-done.1 = bf16[16,16,128]{2,1,0:T(8,128)(2,1)S(1)} async-done(((bf16[16,16,128]{2,1,0:T(8,128)(2,1)}), bf16[16,16,128]{2,1,0:T(8,128)(2,1)S(1)}, u32[]{:S(2)}, u32[]{:S(2)}) %all-to-all-start.1) | async-done | bytes 65568 | tf_op jit(solution)/shard_map/all_to_all | solution.py:156
  36.7 0.0 copy-done.5
  36.7 0.1 multiply_reduce_fusion.1
  36.8 21.9 %all_to_all.26 = f32[32,128,2]{1,2,0:T(2,128)S(1)} all-to-all(f32[32,128,2]{1,2,0:T(2,128)S(1)} %broadcast_in_dim.16), channel_id=1, replica_groups=mesh['seq'=16,'chan'=32] {'chan'}, dimensions={0} | all-to-all | bytes 65536 | tf_op jit(solution)/shard_map/all_to_all | solution.py:166
  58.7 0.1 fusion.1
  58.9 13.0 %all_to_all.27 = bf16[16,16,128]{2,1,0:T(8,128)(2,1)} all-to-all(bf16[16,16,128]{2,1,0:T(8,128)(2,1)S(1)} %bitcast.76), channel_id=1, replica_groups=mesh['seq'=16,'chan'=32] {'seq'}, dimensions={0} | all-to-all | bytes 131072 | tf_op jit(solution)/shard_map/all_to_all | solution.py:152
  71.8 3.4 %shard_map.147 = bf16[16,2,16,128]{3,2,1,0:T(8,128)(2,1)} custom-call(bf16[256,128]{1,0:T(8,128)(2,1)} %bitcast.72, f32[256,256]{1,0:T(8,128)} %get-tuple-element.8.filt_ref, bf16[16,3,16,128]{3,2,1,0:T(8,128)(2,1)} %all_to_all.25.x_ref, f32[256,256]{1,0:T(8,128)} %constant.18.clone.fwd_ref, f32[256,128]{1,0:T(8,128)} %constant.19.clone.inv_ref), custom_call_target="tpu_custom_call" | custom-call | tf_op jit(solution)/shard_map/pallas_call | solution.py:138
  75.2 4.8 %all-to-all-start.4 = ((bf16[16,2,16,128]{3,2,1,0:T(8,128)(2,1)}), bf16[16,2,16,128]{3,2,1,0:T(8,128)(2,1)S(1)}, u32[]{:S(2)}, u32[]{:S(2)}) async-start(bf16[16,2,16,128]{3,2,1,0:T(8,128)(2,1)} %shard_map.147), calls=%async_computation.4 | async-start | bytes 262144 | tf_op jit(solution)/shard_map/all_to_all | solution.py:156
  80.0 0.7 copy.43
  80.7 0.7 copy.42
  81.5 0.7 copy.41
  82.2 6.2 %all-to-all-done.4 = bf16[16,2,16,128]{3,2,1,0:T(8,128)(2,1)S(1)} async-done(((bf16[16,2,16,128]{3,2,1,0:T(8,128)(2,1)}), bf16[16,2,16,128]{3,2,1,0:T(8,128)(2,1)S(1)}, u32[]{:S(2)}, u32[]{:S(2)}) %all-to-all-start.4) | async-done | bytes 131104 | tf_op jit(solution)/shard_map/all_to_all | solution.py:156
  88.5 0.7 copy.45
  89.2 0.7 copy.44
  (10 shorter events, 0.1 us)
Async XLA Ops:
  0.6 1.0 %copy-start = (bf16[128,256]{1,0:T(8,128)(2,1)S(1)}, bf16[128,256]{1,0:T(8,128)(2,1)}, u32[]{:S(2)}) copy-start(bf16[128,256]{1,0:T(8,128)(2,1)} %param.14) | copy-start | bytes 196612
  1.6 0.8 copy-start.1
  24.3 4.6 %copy-start.2 = (bf16[128,256]{1,0:T(8,128)(2,1)S(1)}, bf16[128,256]{1,0:T(8,128)(2,1)}, u32[]{:S(2)}) copy-start(bf16[128,256]{1,0:T(8,128)(2,1)} %param.11) | copy-start | bytes 196612
  24.3 12.4 %all-to-all-start.1 = ((bf16[16,16,128]{2,1,0:T(8,128)(2,1)}), bf16[16,16,128]{2,1,0:T(8,128)(2,1)S(1)}, u32[]{:S(2)}, u32[]{:S(2)}) async-start(bf16[16,16,128]{2,1,0:T(8,128)(2,1)} %bitcast.77), calls=%async_computation.1 | async-start | bytes 131072 | tf_op jit(solution)/shard_map/all_to_all | solution.py:156
  28.9 0.8 copy-start.3
  29.7 0.8 copy-start.4
  30.5 6.1 %copy-start.5 = (f32[256]{0:T(256)S(1)}, f32[256]{0:T(256)}, u32[]{:S(2)}) copy-start(f32[256]{0:T(256)} %param.16) | copy-start | bytes 3076
  75.2 13.2 %all-to-all-start.4 = ((bf16[16,2,16,128]{3,2,1,0:T(8,128)(2,1)}), bf16[16,2,16,128]{3,2,1,0:T(8,128)(2,1)S(1)}, u32[]{:S(2)}, u32[]{:S(2)}) async-start(bf16[16,2,16,128]{3,2,1,0:T(8,128)(2,1)} %shard_map.147), calls=%async_computation.4 | async-start | bytes 262144 | tf_op jit(solution)/shard_map/all_to_all | solution.py:156

commit v5 on v4

--- a/solution.py
+++ b/solution.py
@@ -1,3 +1,4 @@
+import functools
 import math
 
 import numpy as np
@@ -85,11 +86,10 @@
 def forward_kernel(x_ref, fwd_ref, inv_ref, conv_ref, filt_ref, acc_ref):
     blocks, _, chans, tok = x_ref.shape
     rows = blocks * chans
-    inner = x_ref[:, 0, :, :].astype(jnp.float32).reshape(rows, tok)
-    value_rows = x_ref[:, 1, :, :].astype(jnp.float32).reshape(rows, tok)
-    taps = x_ref[:, 2, :, :].astype(jnp.float32).reshape(rows, tok)
+    mixed = x_ref[:, 0, :, :].astype(jnp.float32).reshape(rows, tok)
+    taps = x_ref[:, 1, :, :].astype(jnp.float32).reshape(rows, tok)
     table = fwd_ref[...]
-    data_spec = kdot(inner * value_rows, table)
+    data_spec = kdot(mixed, table)
     filt_spec = kdot(taps, table)
     filt_ref[...] = filt_spec
     half = data_spec.shape[1] // 2
@@ -108,9 +108,9 @@
     conv_ref[chans:, :] = (waveform[chans:, :tok] + waveform[: rows - chans, tok:]).astype(conv_ref.dtype)
 
 
-def backward_kernel(d_ref, filt_ref, x_ref, fwd_ref, inv_ref, out_ref, fol_ref, acc_ref):
-    blocks, _, chans, tok = x_ref.shape
-    rows = blocks * chans
+def backward_kernel(chans, d_ref, filt_ref, fwd_ref, inv_ref, out_ref, fol_ref, acc_ref):
+    rows, tok = d_ref.shape
+    blocks = rows // chans
     dconv = d_ref[...].astype(jnp.float32)
     fol_ref[: rows - chans, :] = dconv[chans:, :]
     fol_ref[rows - chans :, :] = jnp.zeros((chans, tok), jnp.float32)
@@ -127,11 +127,7 @@
         )
         acc_ref[: count * chans, :half] += real
         acc_ref[: count * chans, half:] += imag
-    dmixed = kdot(acc_ref[...], inv_ref[...]).reshape(blocks, chans, tok)
-    inner = x_ref[:, 0, :, :].astype(jnp.float32)
-    value_rows = x_ref[:, 1, :, :].astype(jnp.float32)
-    out_ref[:, 0, :, :] = (dmixed * value_rows).astype(out_ref.dtype)
-    out_ref[:, 1, :, :] = (dmixed * inner).astype(out_ref.dtype)
+    out_ref[...] = kdot(acc_ref[...], inv_ref[...]).astype(out_ref.dtype)
 
 
 def vmem_call(kernel, outs, scratch, *args):
@@ -172,7 +168,9 @@
     parts = lax.axis_size("seq")
     forward_np, inverse_np = dft_tables(half)
 
-    stacked = jnp.stack([inner_gate, values, long_filter], axis=0)
+    inner = inner_gate.astype(jnp.float32)
+    value_rows = values.astype(jnp.float32)
+    stacked = jnp.stack([(inner * value_rows).astype(jnp.bfloat16), long_filter], axis=0)
     chan_in = to_channels(stacked, parts)
     blocks, _, chans, tok = chan_in.shape
     rows = blocks * chans
@@ -209,14 +207,16 @@
     dconv = grad_resid * outer
 
     dconv_c = to_channels(dconv.astype(jnp.bfloat16), parts).reshape(rows, tok)
-    (grads_c,) = vmem_call(
-        backward_kernel,
-        (jax.ShapeDtypeStruct((blocks, 2, chans, tok), jnp.bfloat16),),
+    (dmixed_c,) = vmem_call(
+        functools.partial(backward_kernel, chans),
+        (jax.ShapeDtypeStruct((rows, tok), jnp.bfloat16),),
         [pltpu.VMEM((rows, tok), jnp.float32), pltpu.VMEM((rows, 2 * half), jnp.float32)],
-        dconv_c, filt_spec, chan_in, jnp.asarray(forward_np.T), jnp.asarray(inverse_np[:half].T),
-    )
-    grads = from_channels(grads_c)
-    return (normed, grad_resid.astype(jnp.bfloat16), outer_grad, grads[0], grads[1])
+        dconv_c, filt_spec, jnp.asarray(forward_np.T), jnp.asarray(inverse_np[:half].T),
+    )
+    dmixed = from_channels(dmixed_c.reshape(blocks, chans, tok)).astype(jnp.float32)
+    inner_grad = (dmixed * value_rows).astype(jnp.bfloat16)
+    value_grad = (dmixed * inner).astype(jnp.bfloat16)
+    return (normed, grad_resid.astype(jnp.bfloat16), outer_grad, inner_grad, value_grad)
 
 
 def solution(mesh):

time: 90.6 us -> 88.6 us (0.978)
  blocking collectives: 53.1 us -> 51.5 us
where the time goes in v5:
time: 88.6 us; the launch traced here: 88 us
  blocking collectives  51.5 us (58%)
  waiting for transfers between devices  11.6 us (13%)
  starting transfers between devices  9.67 us (11%)
  local copies, waits for them, and re-layouts  7.43 us (8%)
  Pallas kernels  6.6 us (7%)
    all_to_all x2, blocking collectives, to_channels(): return lax.all_to_all(xt, 'seq', 0, 0)  30.4 us
    all_to_all x1, blocking collectives, chan_sum(): return jnp.sum(lax.all_to_all(spread, 'chan', 0, 0), axis=0)  21.1 us
    all_to_all x2, waiting for transfers between devices, from_channels(): back = lax.all_to_all(xc, 'seq', 0, 0)  11.6 us
    all_to_all x2, starting transfers between devices, from_channels(): back = lax.all_to_all(xc, 'seq', 0, 0)  9.67 us
    unnamed x23, local copies, waits for them, and re-layouts  7.41 us
    pallas_call x2, Pallas kernels, vmem_call(): pl.pallas_call(kernel, out_shape=outs, in_specs=[pl.BlockSpec(memory_spac...  6.6 us
  transfers between devices with their start and end apart: 2, of which 2 were waited for; matrix products, arithmetic and copies ran while one was open for 3% of the time, Pallas kernels for 0%

profile of v5, /device:TPU:2, one launch (start us, length us, event | category | flops | bytes accessed | tf_op | source)
XLA Modules:
  0.0 88.0 jit_solution(9959942602873617990)
XLA Ops:
  0.6 0.0 copy-start
  0.6 1.0 %copy.37 = bf16[128,256]{0,1:T(8,128)(2,1)S(1)} copy(bf16[128,256]{1,0:T(8,128)(2,1)} %param.15) | data formatting | bytes 131072 | tf_op args[4]
  1.6 0.0 copy-done
  1.6 0.0 copy-start.1
  1.6 0.1 copy.36
  1.8 0.7 copy-done.1
  2.5 0.1 copy.35
  2.7 17.4 %all_to_all.25.x_ref = bf16[16,2,16,128]{3,2,1,0:T(8,128)(2,1)} all-to-all(bf16[16,2,16,128]{3,2,1,0:T(8,128)(2,1)S(1)} %bitcast.72), channel_id=1, replica_groups=mesh['seq'=16,'chan'=32] {'seq'}, dimensions={0} | all-to-all | bytes 262144 | tf_op jit(solution)/shard_map/all_to_all | solution.py:148
  20.1 3.3 %shard_map.146 = (bf16[256,128]{1,0:T(8,128)(2,1)}, f32[256,256]{1,0:T(8,128)}) custom-call(bf16[16,2,16,128]{3,2,1,0:T(8,128)(2,1)} %all_to_all.25.x_ref, f32[128,256]{1,0:T(8,128)} %constant.16.clone.fwd_ref, f32[256,256]{1,0:T(8,128)} %constant.17.clone.inv_ref), custom_call_target="tpu_custom_call" | custom-call | tf_op jit(solution)/shard_map/pallas_call | solution.py:134
  23.4 0.0 copy-start.2
  23.4 4.9 %all-to-all-start.1 = ((bf16[16,16,128]{2,1,0:T(8,128)(2,1)}), bf16[16,16,128]{2,1,0:T(8,128)(2,1)S(1)}, u32[]{:S(2)}, u32[]{:S(2)}) async-start(bf16[16,16,128]{2,1,0:T(8,128)(2,1)} %bitcast.77), calls=%async_computation.1 | async-start | bytes 131072 | tf_op jit(solution)/shard_map/all_to_all | solution.py:152
  28.3 0.0 copy-done.2
  28.3 0.0 copy-start.3
  28.3 0.1 copy.34
  28.4 0.7 copy-done.3
  29.1 0.1 copy.33
  29.3 0.7 copy-done.4
  30.0 0.1 copy.39
  30.1 6.0 %all-to-all-done.1 = bf16[16,16,128]{2,1,0:T(8,128)(2,1)S(1)} async-done(((bf16[16,16,128]{2,1,0:T(8,128)(2,1)}), bf16[16,16,128]{2,1,0:T(8,128)(2,1)S(1)}, u32[]{:S(2)}, u32[]{:S(2)}) %all-to-all-start.1) | async-done | bytes 65568 | tf_op jit(solution)/shard_map/all_to_all | solution.py:152
  36.1 0.0 copy-done.5
  36.1 0.1 multiply_reduce_fusion.1
  36.3 21.1 %all_to_all.26 = f32[32,128,2]{1,2,0:T(2,128)S(1)} all-to-all(f32[32,128,2]{1,2,0:T(2,128)S(1)} %broadcast_in_dim.16), channel_id=1, replica_groups=mesh['seq'=16,'chan'=32] {'chan'}, dimensions={0} | all-to-all | bytes 65536 | tf_op jit(solution)/shard_map/all_to_all | solution.py:162
  57.4 0.1 fusion.1
  57.6 13.0 %all_to_all.27 = bf16[16,16,128]{2,1,0:T(8,128)(2,1)} all-to-all(bf16[16,16,128]{2,1,0:T(8,128)(2,1)S(1)} %bitcast.76), channel_id=1, replica_groups=mesh['seq'=16,'chan'=32] {'seq'}, dimensions={0} | all-to-all | bytes 131072 | tf_op jit(solution)/shard_map/all_to_all | solution.py:148
  70.5 3.3 %shard_map.147 = bf16[256,128]{1,0:T(8,128)(2,1)} custom-call(bf16[256,128]{1,0:T(8,128)(2,1)} %bitcast.74, f32[256,256]{1,0:T(8,128)} %get-tuple-element.8.filt_ref, f32[256,256]{1,0:T(8,128)} %constant.18.clone.fwd_ref, f32[256,128]{1,0:T(8,128)} %constant.19.clone.inv_ref), custom_call_target="tpu_custom_call" | custom-call | tf_op jit(solution)/shard_map/pallas_call | solution.py:134
  73.9 4.8 %all-to-all-start.4 = ((bf16[16,16,128]{2,1,0:T(8,128)(2,1)}), bf16[16,16,128]{2,1,0:T(8,128)(2,1)S(1)}, u32[]{:S(2)}, u32[]{:S(2)}) async-start(bf16[16,16,128]{2,1,0:T(8,128)(2,1)} %bitcast.73), calls=%async_computation.4 | async-start | bytes 131072 | tf_op jit(solution)/shard_map/all_to_all | solution.py:152
  78.6 0.7 copy.40
  79.4 0.7 copy.41
  80.1 0.7 copy.42
  80.9 5.6 %all-to-all-done.4 = bf16[16,16,128]{2,1,0:T(8,128)(2,1)S(1)} async-done(((bf16[16,16,128]{2,1,0:T(8,128)(2,1)}), bf16[16,16,128]{2,1,0:T(8,128)(2,1)S(1)}, u32[]{:S(2)}, u32[]{:S(2)}) %all-to-all-start.4) | async-done | bytes 65568 | tf_op jit(solution)/shard_map/all_to_all | solution.py:152
  86.5 0.7 copy.43
  87.2 0.7 copy.44
  (10 shorter events, 0.2 us)
Async XLA Ops:
  0.6 1.0 %copy-start = (bf16[128,256]{1,0:T(8,128)(2,1)S(1)}, bf16[128,256]{1,0:T(8,128)(2,1)}, u32[]{:S(2)}) copy-start(bf16[128,256]{1,0:T(8,128)(2,1)} %param.14) | copy-start | bytes 196612
  1.6 0.8 copy-start.1
  23.4 4.9 %copy-start.2 = (bf16[128,256]{1,0:T(8,128)(2,1)S(1)}, bf16[128,256]{1,0:T(8,128)(2,1)}, u32[]{:S(2)}) copy-start(bf16[128,256]{1,0:T(8,128)(2,1)} %param.12) | copy-start | bytes 196612
  23.4 12.7 %all-to-all-start.1 = ((bf16[16,16,128]{2,1,0:T(8,128)(2,1)}), bf16[16,16,128]{2,1,0:T(8,128)(2,1)S(1)}, u32[]{:S(2)}, u32[]{:S(2)}) async-start(bf16[16,16,128]{2,1,0:T(8,128)(2,1)} %bitcast.77), calls=%async_computation.1 | async-start | bytes 131072 | tf_op jit(solution)/shard_map/all_to_all | solution.py:152
  28.3 0.8 copy-start.3
  29.1 0.8 copy-start.4
  30.0 6.1 %copy-start.5 = (f32[256]{0:T(256)S(1)}, f32[256]{0:T(256)}, u32[]{:S(2)}) copy-start(f32[256]{0:T(256)} %param.16) | copy-start | bytes 3076
  73.9 12.6 %all-to-all-start.4 = ((bf16[16,16,128]{2,1,0:T(8,128)(2,1)}), bf16[16,16,128]{2,1,0:T(8,128)(2,1)S(1)}, u32[]{:S(2)}, u32[]{:S(2)}) async-start(bf16[16,16,128]{2,1,0:T(8,128)(2,1)} %bitcast.73), calls=%async_computation.4 | async-start | bytes 131072 | tf_op jit(solution)/shard_map/all_to_all | solution.py:152

commit v6 on v5

--- a/solution.py
+++ b/solution.py
@@ -130,6 +130,20 @@
     out_ref[...] = kdot(acc_ref[...], inv_ref[...]).astype(out_ref.dtype)
 
 
+def head_kernel(inner_ref, values_ref, filt_ref, out_ref):
+    blocks, _, chans, tok = out_ref.shape
+    mixed = (inner_ref[...].astype(jnp.float32) * values_ref[...].astype(jnp.float32)).astype(jnp.bfloat16)
+    out_ref[:, 0, :, :] = mixed.astype(jnp.float32).T.reshape(blocks, chans, tok).astype(jnp.bfloat16)
+    out_ref[:, 1, :, :] = filt_ref[...].astype(jnp.float32).T.reshape(blocks, chans, tok).astype(jnp.bfloat16)
+
+
+def tail_kernel(d_ref, inner_ref, values_ref, inner_grad_ref, value_grad_ref):
+    blocks, chans, tok = d_ref.shape
+    dmixed = d_ref[...].astype(jnp.float32).reshape(blocks * chans, tok).T
+    inner_grad_ref[...] = (dmixed * values_ref[...].astype(jnp.float32)).astype(inner_grad_ref.dtype)
+    value_grad_ref[...] = (dmixed * inner_ref[...].astype(jnp.float32)).astype(value_grad_ref.dtype)
+
+
 def vmem_call(kernel, outs, scratch, *args):
     return pl.pallas_call(
         kernel,
@@ -168,10 +182,13 @@
     parts = lax.axis_size("seq")
     forward_np, inverse_np = dft_tables(half)
 
-    inner = inner_gate.astype(jnp.float32)
-    value_rows = values.astype(jnp.float32)
-    stacked = jnp.stack([(inner * value_rows).astype(jnp.bfloat16), long_filter], axis=0)
-    chan_in = to_channels(stacked, parts)
+    (stacked,) = vmem_call(
+        head_kernel,
+        (jax.ShapeDtypeStruct((parts, 2, width // parts, half), jnp.bfloat16),),
+        [],
+        inner_gate, values, long_filter,
+    )
+    chan_in = lax.all_to_all(stacked, "seq", 0, 0)
     blocks, _, chans, tok = chan_in.shape
     rows = blocks * chans
     conv_c, filt_spec = vmem_call(
@@ -213,9 +230,16 @@
         [pltpu.VMEM((rows, tok), jnp.float32), pltpu.VMEM((rows, 2 * half), jnp.float32)],
         dconv_c, filt_spec, jnp.asarray(forward_np.T), jnp.asarray(inverse_np[:half].T),
     )
-    dmixed = from_channels(dmixed_c.reshape(blocks, chans, tok)).astype(jnp.float32)
-    inner_grad = (dmixed * value_rows).astype(jnp.bfloat16)
-    value_grad = (dmixed * inner).astype(jnp.bfloat16)
+    dmixed_t = lax.all_to_all(dmixed_c.reshape(blocks, chans, tok), "seq", 0, 0)
+    inner_grad, value_grad = vmem_call(
+        tail_kernel,
+        (
+            jax.ShapeDtypeStruct((half, width), jnp.bfloat16),
+            jax.ShapeDtypeStruct((half, width), jnp.bfloat16),
+        ),
+        [],
+        dmixed_t, inner_gate, values,
+    )
     return (normed, grad_resid.astype(jnp.bfloat16), outer_grad, inner_grad, value_grad)
 
 

time: 88.6 us -> 89.2 us (level)
  Pallas kernels: 6.6 us -> 9.91 us
  local copies, waits for them, and re-layouts: 7.43 us -> 4.63 us
    all_to_all x0 -> x1, blocking collectives: none -> 18.1 us  [body(): chan_in = lax.all_to_all(stacked, 'seq', 0, 0)]
    all_to_all x2 -> x1, blocking collectives: 30.4 us -> 13 us  [to_channels(): return lax.all_to_all(xt, 'seq', 0, 0)]
    all_to_all x0 -> x1, waiting for transfers between devices: none -> 5.58 us  [body(): dmixed_t = lax.all_to_all(dmixed_c.reshape(blocks, chans, tok), 'seq', 0, 0)]
    all_to_all x2 -> x1, waiting for transfers between devices: 11.6 us -> 6 us  [from_channels(): back = lax.all_to_all(xc, 'seq', 0, 0)]
    all_to_all x0 -> x1, starting transfers between devices: none -> 4.77 us  [body(): dmixed_t = lax.all_to_all(dmixed_c.reshape(blocks, chans, tok), 'seq', 0, 0)]
    all_to_all x2 -> x1, starting transfers between devices: 9.67 us -> 5.15 us  [from_channels(): back = lax.all_to_all(xc, 'seq', 0, 0)]
    pallas_call x2 -> x4, Pallas kernels: 6.6 us -> 9.91 us  [vmem_call(): pl.pallas_call(kernel, out_shape=outs, in_specs=[pl.BlockSpec(memory_spac...]
    unnamed x23 -> x16, local copies, waits for them, and re-layouts: 7.41 us -> 4.62 us
where the time goes in v6:
time: 89.2 us; the launch traced here: 88.5 us
  blocking collectives  51.5 us (58%)
  waiting for transfers between devices  11.6 us (13%)
  starting transfers between devices  9.92 us (11%)
  Pallas kernels  9.91 us (11%)
  local copies, waits for them, and re-layouts  4.63 us (5%)
    all_to_all x1, blocking collectives, chan_sum(): return jnp.sum(lax.all_to_all(spread, 'chan', 0, 0), axis=0)  20.4 us
    all_to_all x1, blocking collectives, body(): chan_in = lax.all_to_all(stacked, 'seq', 0, 0)  18.1 us
    all_to_all x1, blocking collectives, to_channels(): return lax.all_to_all(xt, 'seq', 0, 0)  13 us
    pallas_call x4, Pallas kernels, vmem_call(): pl.pallas_call(kernel, out_shape=outs, in_specs=[pl.BlockSpec(memory_spac...  9.91 us
    all_to_all x1, waiting for transfers between devices, from_channels(): back = lax.all_to_all(xc, 'seq', 0, 0)  6 us
    all_to_all x1, waiting for transfers between devices, body(): dmixed_t = lax.all_to_all(dmixed_c.reshape(blocks, chans, tok), 'seq', 0, 0)  5.58 us
    all_to_all x1, starting transfers between devices, from_channels(): back = lax.all_to_all(xc, 'seq', 0, 0)  5.15 us
    all_to_all x1, starting transfers between devices, body(): dmixed_t = lax.all_to_all(dmixed_c.reshape(blocks, chans, tok), 'seq', 0, 0)  4.77 us
  transfers between devices with their start and end apart: 2, of which 2 were waited for; matrix products, arithmetic and copies ran while one was open for 3% of the time, Pallas kernels for 0%

profile of v6, /device:TPU:2, one launch (start us, length us, event | category | flops | bytes accessed | tf_op | source)
XLA Modules:
  0.0 88.5 jit_solution(568932171245461843)
XLA Ops:
  0.6 1.7 %shard_map.146 = bf16[16,2,16,128]{3,2,1,0:T(8,128)(2,1)} custom-call(bf16[128,256]{1,0:T(8,128)(2,1)} %inner_ref.3, bf16[128,256]{1,0:T(8,128)(2,1)} %values_ref.3, bf16[128,256]{1,0:T(8,128)(2,1)} %filt_ref.1), custom_call_target="tpu_custom_call" | custom-call | tf_op jit(solution)/shard_map/pallas_call | solution.py:148
  2.3 18.1 %all_to_all.25.x_ref = bf16[16,2,16,128]{3,2,1,0:T(8,128)(2,1)} all-to-all(bf16[16,2,16,128]{3,2,1,0:T(8,128)(2,1)} %shard_map.146), channel_id=1, replica_groups=mesh['seq'=16,'chan'=32] {'seq'}, dimensions={0} | all-to-all | bytes 262144 | tf_op jit(solution)/shard_map/all_to_all | solution.py:191
  20.4 3.3 %shard_map.147 = (bf16[256,128]{1,0:T(8,128)(2,1)}, f32[256,256]{1,0:T(8,128)}) custom-call(bf16[16,2,16,128]{3,2,1,0:T(8,128)(2,1)} %all_to_all.25.x_ref, f32[128,256]{1,0:T(8,128)} %constant.16.clone.fwd_ref, f32[256,256]{1,0:T(8,128)} %constant.17.clone.inv_ref), custom_call_target="tpu_custom_call" | custom-call | tf_op jit(solution)/shard_map/pallas_call | solution.py:148
  23.6 0.0 copy-start.1
  23.6 5.2 %all-to-all-start.1 = ((bf16[16,16,128]{2,1,0:T(8,128)(2,1)}), bf16[16,16,128]{2,1,0:T(8,128)(2,1)S(1)}, u32[]{:S(2)}, u32[]{:S(2)}) async-start(bf16[16,16,128]{2,1,0:T(8,128)(2,1)} %bitcast.55), calls=%async_computation.1 | async-start | bytes 131072 | tf_op jit(solution)/shard_map/all_to_all | solution.py:166
  28.8 0.0 copy-done.1
  28.8 0.0 copy-start.2
  28.8 0.1 copy.27
  28.9 0.7 copy-done.2
  29.6 0.0 copy-start.3
  29.7 0.1 copy.26
  29.8 0.7 copy-done.3
  30.5 0.0 copy-start.4
  30.5 0.1 copy.28
  30.6 6.0 %all-to-all-done.1 = bf16[16,16,128]{2,1,0:T(8,128)(2,1)S(1)} async-done(((bf16[16,16,128]{2,1,0:T(8,128)(2,1)}), bf16[16,16,128]{2,1,0:T(8,128)(2,1)S(1)}, u32[]{:S(2)}, u32[]{:S(2)}) %all-to-all-start.1) | async-done | bytes 65568 | tf_op jit(solution)/shard_map/all_to_all | solution.py:166
  36.6 0.0 copy-done.4
  36.6 0.1 multiply_reduce_fusion.1
  36.8 20.4 %all_to_all.26 = f32[32,128,2]{1,2,0:T(2,128)S(1)} all-to-all(f32[32,128,2]{1,2,0:T(2,128)S(1)} %broadcast_in_dim.16), channel_id=1, replica_groups=mesh['seq'=16,'chan'=32] {'chan'}, dimensions={0} | all-to-all | bytes 65536 | tf_op jit(solution)/shard_map/all_to_all | solution.py:176
  57.3 0.1 fusion.1
  57.4 13.0 %all_to_all.27 = bf16[16,16,128]{2,1,0:T(8,128)(2,1)} all-to-all(bf16[16,16,128]{2,1,0:T(8,128)(2,1)S(1)} %bitcast.54), channel_id=1, replica_groups=mesh['seq'=16,'chan'=32] {'seq'}, dimensions={0} | all-to-all | bytes 131072 | tf_op jit(solution)/shard_map/all_to_all | solution.py:162
  70.4 3.3 %shard_map.148 = bf16[256,128]{1,0:T(8,128)(2,1)} custom-call(bf16[256,128]{1,0:T(8,128)(2,1)} %bitcast.53, f32[256,256]{1,0:T(8,128)} %get-tuple-element.10.filt_ref, f32[256,256]{1,0:T(8,128)} %constant.18.clone.fwd_ref, f32[256,128]{1,0:T(8,128)} %constant.19.clone.inv_ref), custom_call_target="tpu_custom_call" | custom-call | tf_op jit(solution)/shard_map/pallas_call | solution.py:148
  73.7 4.8 %all-to-all-start.4 = ((bf16[16,16,128]{2,1,0:T(8,128)(2,1)}), bf16[16,16,128]{2,1,0:T(8,128)(2,1)S(1)}, u32[]{:S(2)}, u32[]{:S(2)}) async-start(bf16[16,16,128]{2,1,0:T(8,128)(2,1)} %bitcast.52), calls=%async_computation.4 | async-start | bytes 131072 | tf_op jit(solution)/shard_map/all_to_all | solution.py:233
  78.4 0.7 copy.29
  79.2 0.7 copy.30
  79.9 0.7 copy.31
  80.7 5.6 %all-to-all-done.4.d_ref = bf16[16,16,128]{2,1,0:T(8,128)(2,1)S(1)} async-done(((bf16[16,16,128]{2,1,0:T(8,128)(2,1)}), bf16[16,16,128]{2,1,0:T(8,128)(2,1)S(1)}, u32[]{:S(2)}, u32[]{:S(2)}) %all-to-all-start.4) | async-done | bytes 65568 | tf_op jit(solution)/shard_map/all_to_all | solution.py:233
  86.2 0.0 copy-start
  86.2 0.6 copy-done
  86.9 1.7 %shard_map.149 = (bf16[128,256]{1,0:T(8,128)(2,1)}, bf16[128,256]{1,0:T(8,128)(2,1)}) custom-call(bf16[16,16,128]{2,1,0:T(8,128)(2,1)} %copy-done, bf16[128,256]{1,0:T(8,128)(2,1)} %inner_ref.3, bf16[128,256]{1,0:T(8,128)(2,1)} %values_ref.3), custom_call_target="tpu_custom_call" | custom-call | tf_op jit(solution)/shard_map/pallas_call | solution.py:148
  (4 shorter events, 0.1 us)
Async XLA Ops:
  23.6 5.2 %copy-start.1 = (bf16[128,256]{1,0:T(8,128)(2,1)S(1)}, bf16[128,256]{1,0:T(8,128)(2,1)}, u32[]{:S(2)}) copy-start(bf16[128,256]{1,0:T(8,128)(2,1)} %param.12) | copy-start | bytes 196612
  23.6 13.0 %all-to-all-start.1 = ((bf16[16,16,128]{2,1,0:T(8,128)(2,1)}), bf16[16,16,128]{2,1,0:T(8,128)(2,1)S(1)}, u32[]{:S(2)}, u32[]{:S(2)}) async-start(bf16[16,16,128]{2,1,0:T(8,128)(2,1)} %bitcast.55), calls=%async_computation.1 | async-start | bytes 131072 | tf_op jit(solution)/shard_map/all_to_all | solution.py:166
  28.8 0.8 copy-start.2
  29.6 0.8 copy-start.3
  30.5 6.1 %copy-start.4 = (f32[256]{0:T(256)S(1)}, f32[256]{0:T(256)}, u32[]{:S(2)}) copy-start(f32[256]{0:T(256)} %param.16) | copy-start | bytes 3076
  73.7 12.6 %all-to-all-start.4 = ((bf16[16,16,128]{2,1,0:T(8,128)(2,1)}), bf16[16,16,128]{2,1,0:T(8,128)(2,1)S(1)}, u32[]{:S(2)}, u32[]{:S(2)}) async-start(bf16[16,16,128]{2,1,0:T(8,128)(2,1)} %bitcast.52), calls=%async_computation.4 | async-start | bytes 131072 | tf_op jit(solution)/shard_map/all_to_all | solution.py:233
  86.2 0.6 copy-start

commit v7 on v5

--- a/solution.py
+++ b/solution.py
@@ -58,75 +58,69 @@
     )
 
 
-def packed_product(left, right, conjugate):
-    half = left.shape[-1] // 2
-    left_real, left_imag = (left[:, :half], left[:, half:])
-    right_real, right_imag = (right[:, :half], right[:, half:])
-    first_bin = lax.broadcasted_iota(jnp.int32, left_real.shape, 1) == 0
-    if conjugate:
-        right_eff = jnp.where(first_bin, right_imag, -right_imag)
-    else:
-        right_eff = right_imag
-    real_out = left_real * right_real - jnp.where(first_bin, 0.0, left_imag * right_eff)
-    imag_out = jnp.where(
-        first_bin, left_imag * right_imag, left_real * right_eff + left_imag * right_real
-    )
-    return real_out, imag_out
-
-
 def kdot(left, right):
-    return jnp.dot(left, right, precision=HIGHEST_MODE, preferred_element_type=jnp.float32)
-
-
-def tiled_rows(part, count):
-    rows, lanes = part.shape
-    return jnp.broadcast_to(part[None], (count, rows, lanes)).reshape(count * rows, lanes)
-
-
-def forward_kernel(x_ref, fwd_ref, inv_ref, conv_ref, filt_ref, acc_ref):
+    return jnp.dot(left, right, precision=lax.Precision.HIGH, preferred_element_type=jnp.float32)
+
+
+def split_taps(filt_spec, fr_ref, ff_ref, fm_ref):
+    half = filt_spec.shape[1] // 2
+    real, imag = filt_spec[:, :half], filt_spec[:, half:]
+    first_bin = lax.broadcasted_iota(jnp.int32, real.shape, 1) == 0
+    fr_ref[...] = real
+    ff_ref[...] = jnp.where(first_bin, imag, real)
+    fm_ref[...] = jnp.where(first_bin, 0.0, imag)
+
+
+def block_terms(spec_ref, fr_ref, ff_ref, fm_ref, acc_ref, chans, pairs, conjugate):
+    half = acc_ref.shape[1] // 2
+    for out, terms in pairs:
+        acc_real = jnp.zeros((chans, half), jnp.float32)
+        acc_imag = jnp.zeros((chans, half), jnp.float32)
+        for src, lag in terms:
+            rows = pl.ds(src * chans, chans)
+            taps = pl.ds(lag * chans, chans)
+            left_real = spec_ref[rows, pl.ds(0, half)]
+            left_imag = spec_ref[rows, pl.ds(half, half)]
+            right_real = fr_ref[taps, :]
+            right_first = ff_ref[taps, :]
+            right_masked = fm_ref[taps, :]
+            if conjugate:
+                acc_real = acc_real + (left_real * right_real + left_imag * right_masked)
+                acc_imag = acc_imag + (left_imag * right_first - left_real * right_masked)
+            else:
+                acc_real = acc_real + (left_real * right_real - left_imag * right_masked)
+                acc_imag = acc_imag + (left_real * right_masked + left_imag * right_first)
+        acc_ref[pl.ds(out * chans, chans), pl.ds(0, half)] = acc_real
+        acc_ref[pl.ds(out * chans, chans), pl.ds(half, half)] = acc_imag
+
+
+def forward_kernel(x_ref, fwd_ref, inv_ref, conv_ref, filt_ref, spec_ref, fr_ref, ff_ref, fm_ref, acc_ref):
     blocks, _, chans, tok = x_ref.shape
     rows = blocks * chans
     mixed = x_ref[:, 0, :, :].astype(jnp.float32).reshape(rows, tok)
     taps = x_ref[:, 1, :, :].astype(jnp.float32).reshape(rows, tok)
     table = fwd_ref[...]
-    data_spec = kdot(mixed, table)
+    spec_ref[...] = kdot(mixed, table)
     filt_spec = kdot(taps, table)
     filt_ref[...] = filt_spec
-    half = data_spec.shape[1] // 2
-    real0, imag0 = packed_product(data_spec, tiled_rows(filt_spec[0:chans], blocks), False)
-    acc_ref[:, :half] = real0
-    acc_ref[:, half:] = imag0
-    for lag in range(1, blocks):
-        count = blocks - lag
-        real, imag = packed_product(
-            data_spec[: count * chans], tiled_rows(filt_spec[lag * chans : (lag + 1) * chans], count), False
-        )
-        acc_ref[lag * chans :, :half] += real
-        acc_ref[lag * chans :, half:] += imag
+    split_taps(filt_spec, fr_ref, ff_ref, fm_ref)
+    pairs = [(out, [(out - lag, lag) for lag in range(out + 1)]) for out in range(blocks)]
+    block_terms(spec_ref, fr_ref, ff_ref, fm_ref, acc_ref, chans, pairs, False)
     waveform = kdot(acc_ref[...], inv_ref[...])
     conv_ref[0:chans, :] = waveform[0:chans, :tok].astype(conv_ref.dtype)
     conv_ref[chans:, :] = (waveform[chans:, :tok] + waveform[: rows - chans, tok:]).astype(conv_ref.dtype)
 
 
-def backward_kernel(chans, d_ref, filt_ref, fwd_ref, inv_ref, out_ref, fol_ref, acc_ref):
+def backward_kernel(chans, d_ref, filt_ref, fwd_ref, inv_ref, out_ref, fol_ref, spec_ref, fr_ref, ff_ref, fm_ref, acc_ref):
     rows, tok = d_ref.shape
     blocks = rows // chans
     dconv = d_ref[...].astype(jnp.float32)
     fol_ref[: rows - chans, :] = dconv[chans:, :]
     fol_ref[rows - chans :, :] = jnp.zeros((chans, tok), jnp.float32)
-    back_spec = kdot(dconv, fwd_ref[:tok, :]) + kdot(fol_ref[...], fwd_ref[tok:, :])
-    filt_spec = filt_ref[...]
-    half = back_spec.shape[1] // 2
-    real0, imag0 = packed_product(back_spec, tiled_rows(filt_spec[0:chans], blocks), True)
-    acc_ref[:, :half] = real0
-    acc_ref[:, half:] = imag0
-    for lag in range(1, blocks):
-        count = blocks - lag
-        real, imag = packed_product(
-            back_spec[lag * chans :], tiled_rows(filt_spec[lag * chans : (lag + 1) * chans], count), True
-        )
-        acc_ref[: count * chans, :half] += real
-        acc_ref[: count * chans, half:] += imag
+    spec_ref[...] = kdot(dconv, fwd_ref[:tok, :]) + kdot(fol_ref[...], fwd_ref[tok:, :])
+    split_taps(filt_ref[...], fr_ref, ff_ref, fm_ref)
+    pairs = [(out, [(out + lag, lag) for lag in range(blocks - out)]) for out in range(blocks)]
+    block_terms(spec_ref, fr_ref, ff_ref, fm_ref, acc_ref, chans, pairs, True)
     out_ref[...] = kdot(acc_ref[...], inv_ref[...]).astype(out_ref.dtype)
 
 
@@ -180,7 +174,9 @@
             jax.ShapeDtypeStruct((rows, tok), jnp.bfloat16),
             jax.ShapeDtypeStruct((rows, 2 * half), jnp.float32),
         ),
-        [pltpu.VMEM((rows, 2 * half), jnp.float32)],
+        [pltpu.VMEM((rows, 2 * half), jnp.float32)]
+        + [pltpu.VMEM((rows, half), jnp.float32) for _ in range(3)]
+        + [pltpu.VMEM((rows, 2 * half), jnp.float32)],
         chan_in, jnp.asarray(forward_np[:, :half].T), jnp.asarray(inverse_np.T),
     )
     conv_c = conv_c.reshape(blocks, chans, tok)
@@ -210,7 +206,9 @@
     (dmixed_c,) = vmem_call(
         functools.partial(backward_kernel, chans),
         (jax.ShapeDtypeStruct((rows, tok), jnp.bfloat16),),
-        [pltpu.VMEM((rows, tok), jnp.float32), pltpu.VMEM((rows, 2 * half), jnp.float32)],
+        [pltpu.VMEM((rows, tok), jnp.float32), pltpu.VMEM((rows, 2 * half), jnp.float32)]
+        + [pltpu.VMEM((rows, half), jnp.float32) for _ in range(3)]
+        + [pltpu.VMEM((rows, 2 * half), jnp.float32)],
         dconv_c, filt_spec, jnp.asarray(forward_np.T), jnp.asarray(inverse_np[:half].T),
     )
     dmixed = from_channels(dmixed_c.reshape(blocks, chans, tok)).astype(jnp.float32)

time: 88.6 us -> 87.3 us (0.985)
  Pallas kernels: 6.6 us -> 5.38 us
    pallas_call x2, Pallas kernels: 6.6 us -> 5.38 us  [vmem_call(): pl.pallas_call(kernel, out_shape=outs, in_specs=[pl.BlockSpec(memory_spac...]
where the time goes in v7:
time: 87.3 us; the launch traced here: 86.7 us
  blocking collectives  51.5 us (59%)
  waiting for transfers between devices  11.6 us (13%)
  starting transfers between devices  9.67 us (11%)
  local copies, waits for them, and re-layouts  7.43 us (9%)
  Pallas kernels  5.38 us (6%)
    all_to_all x2, blocking collectives, to_channels(): return lax.all_to_all(xt, 'seq', 0, 0)  30.4 us
    all_to_all x1, blocking collectives, chan_sum(): return jnp.sum(lax.all_to_all(spread, 'chan', 0, 0), axis=0)  21.1 us
    all_to_all x2, waiting for transfers between devices, from_channels(): back = lax.all_to_all(xc, 'seq', 0, 0)  11.6 us
    all_to_all x2, starting transfers between devices, from_channels(): back = lax.all_to_all(xc, 'seq', 0, 0)  9.67 us
    unnamed x23, local copies, waits for them, and re-layouts  7.41 us
    pallas_call x2, Pallas kernels, vmem_call(): pl.pallas_call(kernel, out_shape=outs, in_specs=[pl.BlockSpec(memory_spac...  5.38 us
  transfers between devices with their start and end apart: 2, of which 2 were waited for; matrix products, arithmetic and copies ran while one was open for 3% of the time, Pallas kernels for 0%

profile of v7, /device:TPU:2, one launch (start us, length us, event | category | flops | bytes accessed | tf_op | source)
XLA Modules:
  0.0 86.7 jit_solution(14877156387410397689)
XLA Ops:
  0.6 0.0 copy-start
  0.6 1.0 %copy.37 = bf16[128,256]{0,1:T(8,128)(2,1)S(1)} copy(bf16[128,256]{1,0:T(8,128)(2,1)} %param.15) | data formatting | bytes 131072 | tf_op args[4]
  1.6 0.0 copy-done
  1.6 0.0 copy-start.1
  1.6 0.1 copy.36
  1.8 0.7 copy-done.1
  2.5 0.1 copy.35
  2.7 17.4 %all_to_all.25.x_ref = bf16[16,2,16,128]{3,2,1,0:T(8,128)(2,1)} all-to-all(bf16[16,2,16,128]{3,2,1,0:T(8,128)(2,1)S(1)} %bitcast.72), channel_id=1, replica_groups=mesh['seq'=16,'chan'=32] {'seq'}, dimensions={0} | all-to-all | bytes 262144 | tf_op jit(solution)/shard_map/all_to_all | solution.py:142
  20.1 2.7 %shard_map.146 = (bf16[256,128]{1,0:T(8,128)(2,1)}, f32[256,256]{1,0:T(8,128)}) custom-call(bf16[16,2,16,128]{3,2,1,0:T(8,128)(2,1)} %all_to_all.25.x_ref, f32[128,256]{1,0:T(8,128)} %constant.16.clone.fwd_ref, f32[256,256]{1,0:T(8,128)} %constant.17.clone.inv_ref), custom_call_target="tpu_custom_call" | custom-call | tf_op jit(solution)/shard_map/pallas_call | solution.py:128
  22.8 0.0 copy-start.2
  22.8 4.9 %all-to-all-start.1 = ((bf16[16,16,128]{2,1,0:T(8,128)(2,1)}), bf16[16,16,128]{2,1,0:T(8,128)(2,1)S(1)}, u32[]{:S(2)}, u32[]{:S(2)}) async-start(bf16[16,16,128]{2,1,0:T(8,128)(2,1)} %bitcast.77), calls=%async_computation.1 | async-start | bytes 131072 | tf_op jit(solution)/shard_map/all_to_all | solution.py:146
  27.7 0.0 copy-done.2
  27.7 0.0 copy-start.3
  27.7 0.1 copy.34
  27.8 0.7 copy-done.3
  28.6 0.1 copy.33
  28.7 0.7 copy-done.4
  29.4 0.1 copy.39
  29.5 6.0 %all-to-all-done.1 = bf16[16,16,128]{2,1,0:T(8,128)(2,1)S(1)} async-done(((bf16[16,16,128]{2,1,0:T(8,128)(2,1)}), bf16[16,16,128]{2,1,0:T(8,128)(2,1)S(1)}, u32[]{:S(2)}, u32[]{:S(2)}) %all-to-all-start.1) | async-done | bytes 65568 | tf_op jit(solution)/shard_map/all_to_all | solution.py:146
  35.5 0.0 copy-done.5
  35.5 0.1 multiply_reduce_fusion.1
  35.7 21.1 %all_to_all.26 = f32[32,128,2]{1,2,0:T(2,128)S(1)} all-to-all(f32[32,128,2]{1,2,0:T(2,128)S(1)} %broadcast_in_dim.16), channel_id=1, replica_groups=mesh['seq'=16,'chan'=32] {'chan'}, dimensions={0} | all-to-all | bytes 65536 | tf_op jit(solution)/shard_map/all_to_all | solution.py:156
  56.9 0.1 fusion.1
  57.0 13.0 %all_to_all.27 = bf16[16,16,128]{2,1,0:T(8,128)(2,1)} all-to-all(bf16[16,16,128]{2,1,0:T(8,128)(2,1)S(1)} %bitcast.76), channel_id=1, replica_groups=mesh['seq'=16,'chan'=32] {'seq'}, dimensions={0} | all-to-all | bytes 131072 | tf_op jit(solution)/shard_map/all_to_all | solution.py:142
  70.0 2.7 %shard_map.147 = bf16[256,128]{1,0:T(8,128)(2,1)} custom-call(bf16[256,128]{1,0:T(8,128)(2,1)} %bitcast.74, f32[256,256]{1,0:T(8,128)} %get-tuple-element.8.filt_ref, f32[256,256]{1,0:T(8,128)} %constant.18.clone.fwd_ref, f32[256,128]{1,0:T(8,128)} %constant.19.clone.inv_ref), custom_call_target="tpu_custom_call" | custom-call | tf_op jit(solution)/shard_map/pallas_call | solution.py:128
  72.6 4.8 %all-to-all-start.4 = ((bf16[16,16,128]{2,1,0:T(8,128)(2,1)}), bf16[16,16,128]{2,1,0:T(8,128)(2,1)S(1)}, u32[]{:S(2)}, u32[]{:S(2)}) async-start(bf16[16,16,128]{2,1,0:T(8,128)(2,1)} %bitcast.73), calls=%async_computation.4 | async-start | bytes 131072 | tf_op jit(solution)/shard_map/all_to_all | solution.py:146
  77.4 0.7 copy.40
  78.2 0.7 copy.41
  78.9 0.7 copy.42
  79.6 5.6 %all-to-all-done.4 = bf16[16,16,128]{2,1,0:T(8,128)(2,1)S(1)} async-done(((bf16[16,16,128]{2,1,0:T(8,128)(2,1)}), bf16[16,16,128]{2,1,0:T(8,128)(2,1)S(1)}, u32[]{:S(2)}, u32[]{:S(2)}) %all-to-all-start.4) | async-done | bytes 65568 | tf_op jit(solution)/shard_map/all_to_all | solution.py:146
  85.3 0.7 copy.43
  86.0 0.7 copy.44
  (10 shorter events, 0.2 us)
Async XLA Ops:
  0.6 1.0 %copy-start = (bf16[128,256]{1,0:T(8,128)(2,1)S(1)}, bf16[128,256]{1,0:T(8,128)(2,1)}, u32[]{:S(2)}) copy-start(bf16[128,256]{1,0:T(8,128)(2,1)} %param.14) | copy-start | bytes 196612
  1.6 0.8 copy-start.1
  22.8 4.9 %copy-start.2 = (bf16[128,256]{1,0:T(8,128)(2,1)S(1)}, bf16[128,256]{1,0:T(8,128)(2,1)}, u32[]{:S(2)}) copy-start(bf16[128,256]{1,0:T(8,128)(2,1)} %param.12) | copy-start | bytes 196612
  22.8 12.7 %all-to-all-start.1 = ((bf16[16,16,128]{2,1,0:T(8,128)(2,1)}), bf16[16,16,128]{2,1,0:T(8,128)(2,1)S(1)}, u32[]{:S(2)}, u32[]{:S(2)}) async-start(bf16[16,16,128]{2,1,0:T(8,128)(2,1)} %bitcast.77), calls=%async_computation.1 | async-start | bytes 131072 | tf_op jit(solution)/shard_map/all_to_all | solution.py:146
  27.7 0.8 copy-start.3
  28.6 0.8 copy-start.4
  29.4 6.1 %copy-start.5 = (f32[256]{0:T(256)S(1)}, f32[256]{0:T(256)}, u32[]{:S(2)}) copy-start(f32[256]{0:T(256)} %param.16) | copy-start | bytes 3076
  72.6 12.6 %all-to-all-start.4 = ((bf16[16,16,128]{2,1,0:T(8,128)(2,1)}), bf16[16,16,128]{2,1,0:T(8,128)(2,1)S(1)}, u32[]{:S(2)}, u32[]{:S(2)}) async-start(bf16[16,16,128]{2,1,0:T(8,128)(2,1)} %bitcast.73), calls=%async_computation.4 | async-start | bytes 131072 | tf_op jit(solution)/shard_map/all_to_all | solution.py:146

commit v8 on v7

--- a/solution.py
+++ b/solution.py
@@ -164,8 +164,16 @@
 
     inner = inner_gate.astype(jnp.float32)
     value_rows = values.astype(jnp.float32)
-    stacked = jnp.stack([(inner * value_rows).astype(jnp.bfloat16), long_filter], axis=0)
-    chan_in = to_channels(stacked, parts)
+    eye = jnp.eye(width, dtype=jnp.bfloat16)
+
+    def flipped(x):
+        return lax.dot_general(eye, x, (((1,), (1,)), ((), ())), preferred_element_type=jnp.float32)
+
+    stacked = jnp.stack(
+        [flipped((inner * value_rows).astype(jnp.bfloat16)), flipped(long_filter)], axis=0
+    ).astype(jnp.bfloat16)
+    stacked = jnp.moveaxis(stacked.reshape(2, parts, width // parts, half), 1, 0)
+    chan_in = lax.all_to_all(stacked, "seq", 0, 0)
     blocks, _, chans, tok = chan_in.shape
     rows = blocks * chans
     conv_c, filt_spec = vmem_call(
@@ -211,7 +219,8 @@
         + [pltpu.VMEM((rows, 2 * half), jnp.float32)],
         dconv_c, filt_spec, jnp.asarray(forward_np.T), jnp.asarray(inverse_np[:half].T),
     )
-    dmixed = from_channels(dmixed_c.reshape(blocks, chans, tok)).astype(jnp.float32)
+    dmixed_t = lax.all_to_all(dmixed_c.reshape(blocks, chans, tok), "seq", 0, 0).reshape(width, tok)
+    dmixed = lax.dot_general(dmixed_t, eye, (((0,), (0,)), ((), ())), preferred_element_type=jnp.float32)
     inner_grad = (dmixed * value_rows).astype(jnp.bfloat16)
     value_grad = (dmixed * inner).astype(jnp.bfloat16)
     return (normed, grad_resid.astype(jnp.bfloat16), outer_grad, inner_grad, value_grad)

time: 87.3 us -> 85.8 us (0.983)
  local copies, waits for them, and re-layouts: 7.43 us -> 4.84 us
  matrix products: 0 us -> 1.22 us
    all_to_all x2 -> x1, blocking collectives: 30.4 us -> 13 us  [to_channels(): return lax.all_to_all(xt, 'seq', 0, 0)]
    all_to_all x0 -> x1, blocking collectives: none -> 17.4 us  [body(): chan_in = lax.all_to_all(stacked, 'seq', 0, 0)]
    all_to_all x0 -> x1, waiting for transfers between devices: none -> 5.58 us  [body(): lax.all_to_all(dmixed_c.reshape(blocks, chans, tok), 'seq', 0, 0)]
    all_to_all x2 -> x1, waiting for transfers between devices: 11.6 us -> 6 us  [from_channels(): back = lax.all_to_all(xc, 'seq', 0, 0)]
    all_to_all x0 -> x1, starting transfers between devices: none -> 4.77 us  [body(): lax.all_to_all(dmixed_c.reshape(blocks, chans, tok), 'seq', 0, 0)]
    all_to_all x2 -> x1, starting transfers between devices: 9.67 us -> 4.91 us  [from_channels(): back = lax.all_to_all(xc, 'seq', 0, 0)]
    unnamed x23 -> x20, local copies, waits for them, and re-layouts: 7.41 us -> 4.83 us
    dot_general x0 -> x3, matrix products: none -> 1.22 us  [the longest x1 0.85 us: body(): lax.dot_general(dmixed_t, eye, (((0,), (0,)), ((), ())), preferred_elemen...]
where the time goes in v8:
time: 85.8 us; the launch traced here: 85.3 us
  blocking collectives  51.5 us (60%)
  waiting for transfers between devices  11.6 us (14%)
  starting transfers between devices  9.68 us (11%)
  Pallas kernels  5.38 us (6%)
  local copies, waits for them, and re-layouts  4.84 us (6%)
  matrix products  1.22 us (1%)
    all_to_all x1, blocking collectives, chan_sum(): return jnp.sum(lax.all_to_all(spread, 'chan', 0, 0), axis=0)  21.1 us
    all_to_all x1, blocking collectives, body(): chan_in = lax.all_to_all(stacked, 'seq', 0, 0)  17.4 us
    all_to_all x1, blocking collectives, to_channels(): return lax.all_to_all(xt, 'seq', 0, 0)  13 us
    all_to_all x1, waiting for transfers between devices, from_channels(): back = lax.all_to_all(xc, 'seq', 0, 0)  6 us
    all_to_all x1, waiting for transfers between devices, body(): lax.all_to_all(dmixed_c.reshape(blocks, chans, tok), 'seq', 0, 0)  5.58 us
    pallas_call x2, Pallas kernels, vmem_call(): pl.pallas_call(kernel, out_shape=outs, in_specs=[pl.BlockSpec(memory_spac...  5.38 us
    all_to_all x1, starting transfers between devices, from_channels(): back = lax.all_to_all(xc, 'seq', 0, 0)  4.91 us
    unnamed x20, local copies, waits for them, and re-layouts  4.83 us
  transfers between devices with their start and end apart: 2, of which 2 were waited for; matrix products, arithmetic and copies ran while one was open for 3% of the time, Pallas kernels for 0%

profile of v8, /device:TPU:2, one launch (start us, length us, event | category | flops | bytes accessed | tf_op | source)
XLA Modules:
  0.0 85.3 jit_solution(10233903652286075508)
XLA Ops:
  0.6 0.0 copy-start
  0.6 0.0 copy-start.1
  0.7 0.0 copy-start.2
  0.7 0.8 copy-done
  1.5 0.2 convolution_convert_fusion
  1.7 0.0 copy-done.1
  1.7 0.0 copy-done.2
  1.7 0.2 convolution_convert_fusion.1
  1.9 17.4 %all_to_all.25.x_ref = bf16[16,2,16,128]{3,2,1,0:T(8,128)(2,1)} all-to-all(bf16[16,2,16,128]{3,2,1,0:T(8,128)(2,1)S(1)} %maximum_bitcast_fusion), channel_id=1, replica_groups=mesh['seq'=16,'chan'=32] {'seq'}, dimensions={0} | all-to-all | bytes 262144 | tf_op jit(solution)/shard_map/all_to_all | solution.py:176
  19.3 2.7 %shard_map.146 = (bf16[256,128]{1,0:T(8,128)(2,1)}, f32[256,256]{1,0:T(8,128)}) custom-call(bf16[16,2,16,128]{3,2,1,0:T(8,128)(2,1)} %all_to_all.25.x_ref, f32[128,256]{1,0:T(8,128)} %constant.16.clone.fwd_ref, f32[256,256]{1,0:T(8,128)} %constant.17.clone.inv_ref), custom_call_target="tpu_custom_call" | custom-call | tf_op jit(solution)/shard_map/pallas_call | solution.py:128
  22.0 0.0 copy-start.3
  22.0 4.9 %all-to-all-start.1 = ((bf16[16,16,128]{2,1,0:T(8,128)(2,1)}), bf16[16,16,128]{2,1,0:T(8,128)(2,1)S(1)}, u32[]{:S(2)}, u32[]{:S(2)}) async-start(bf16[16,16,128]{2,1,0:T(8,128)(2,1)} %bitcast.63), calls=%async_computation.1 | async-start | bytes 131072 | tf_op jit(solution)/shard_map/all_to_all | solution.py:146
  26.9 0.0 copy-done.3
  27.0 0.0 copy-start.4
  27.0 0.1 copy.27
  27.1 0.7 copy-done.4
  27.8 0.1 copy.26
  27.9 0.7 copy-done.5
  28.6 0.1 copy.28
  28.8 6.0 %all-to-all-done.1 = bf16[16,16,128]{2,1,0:T(8,128)(2,1)S(1)} async-done(((bf16[16,16,128]{2,1,0:T(8,128)(2,1)}), bf16[16,16,128]{2,1,0:T(8,128)(2,1)S(1)}, u32[]{:S(2)}, u32[]{:S(2)}) %all-to-all-start.1) | async-done | bytes 65568 | tf_op jit(solution)/shard_map/all_to_all | solution.py:146
  34.7 0.0 copy-done.6
  34.8 0.1 multiply_reduce_fusion.1
  34.9 21.1 %all_to_all.26 = f32[32,128,2]{1,2,0:T(2,128)S(1)} all-to-all(f32[32,128,2]{1,2,0:T(2,128)S(1)} %broadcast_in_dim.16), channel_id=1, replica_groups=mesh['seq'=16,'chan'=32] {'chan'}, dimensions={0} | all-to-all | bytes 65536 | tf_op jit(solution)/shard_map/all_to_all | solution.py:156
  56.1 0.1 fusion.2
  56.2 13.0 %all_to_all.27 = bf16[16,16,128]{2,1,0:T(8,128)(2,1)} all-to-all(bf16[16,16,128]{2,1,0:T(8,128)(2,1)S(1)} %bitcast.62), channel_id=1, replica_groups=mesh['seq'=16,'chan'=32] {'seq'}, dimensions={0} | all-to-all | bytes 131072 | tf_op jit(solution)/shard_map/all_to_all | solution.py:142
  69.2 2.7 %shard_map.147 = bf16[256,128]{1,0:T(8,128)(2,1)} custom-call(bf16[256,128]{1,0:T(8,128)(2,1)} %bitcast.61, f32[256,256]{1,0:T(8,128)} %get-tuple-element.8.filt_ref, f32[256,256]{1,0:T(8,128)} %constant.18.clone.fwd_ref, f32[256,128]{1,0:T(8,128)} %constant.19.clone.inv_ref), custom_call_target="tpu_custom_call" | custom-call | tf_op jit(solution)/shard_map/pallas_call | solution.py:128
  71.9 4.8 %all-to-all-start.4 = ((bf16[16,16,128]{2,1,0:T(8,128)(2,1)}), bf16[16,16,128]{2,1,0:T(8,128)(2,1)S(1)}, u32[]{:S(2)}, u32[]{:S(2)}) async-start(bf16[16,16,128]{2,1,0:T(8,128)(2,1)} %bitcast.60), calls=%async_computation.4 | async-start | bytes 131072 | tf_op jit(solution)/shard_map/all_to_all | solution.py:222
  76.6 0.7 copy.29
  77.4 0.7 copy.30
  78.1 0.7 copy.31
  78.9 5.6 %all-to-all-done.4 = bf16[16,16,128]{2,1,0:T(8,128)(2,1)S(1)} async-done(((bf16[16,16,128]{2,1,0:T(8,128)(2,1)}), bf16[16,16,128]{2,1,0:T(8,128)(2,1)S(1)}, u32[]{:S(2)}, u32[]{:S(2)}) %all-to-all-start.4) | async-done | bytes 65568 | tf_op jit(solution)/shard_map/all_to_all | solution.py:222
  84.4 0.9 fusion.3
  (7 shorter events, 0.1 us)
Async XLA Ops:
  0.6 0.8 copy-start
  0.6 1.0 %copy-start.1 = (bf16[128,256]{1,0:T(8,128)(2,1)S(1)}, bf16[128,256]{1,0:T(8,128)(2,1)}, u32[]{:S(2)}) copy-start(bf16[128,256]{1,0:T(8,128)(2,1)} %param.14) | copy-start | bytes 196612
  0.7 1.0 %copy-start.2 = (bf16[128,256]{1,0:T(8,128)(2,1)S(1)}, bf16[128,256]{1,0:T(8,128)(2,1)}, u32[]{:S(2)}) copy-start(bf16[128,256]{1,0:T(8,128)(2,1)} %param.13) | copy-start | bytes 196612
  22.0 4.9 %copy-start.3 = (bf16[128,256]{1,0:T(8,128)(2,1)S(1)}, bf16[128,256]{1,0:T(8,128)(2,1)}, u32[]{:S(2)}) copy-start(bf16[128,256]{1,0:T(8,128)(2,1)} %param.12) | copy-start | bytes 196612
  22.0 12.7 %all-to-all-start.1 = ((bf16[16,16,128]{2,1,0:T(8,128)(2,1)}), bf16[16,16,128]{2,1,0:T(8,128)(2,1)S(1)}, u32[]{:S(2)}, u32[]{:S(2)}) async-start(bf16[16,16,128]{2,1,0:T(8,128)(2,1)} %bitcast.63), calls=%async_computation.1 | async-start | bytes 131072 | tf_op jit(solution)/shard_map/all_to_all | solution.py:146
  27.0 0.8 copy-start.4
  27.8 0.8 copy-start.5
  28.6 6.1 %copy-start.6 = (f32[256]{0:T(256)S(1)}, f32[256]{0:T(256)}, u32[]{:S(2)}) copy-start(f32[256]{0:T(256)} %param.16) | copy-start | bytes 3076
  71.9 12.6 %all-to-all-start.4 = ((bf16[16,16,128]{2,1,0:T(8,128)(2,1)}), bf16[16,16,128]{2,1,0:T(8,128)(2,1)S(1)}, u32[]{:S(2)}, u32[]{:S(2)}) async-start(bf16[16,16,128]{2,1,0:T(8,128)(2,1)} %bitcast.60), calls=%async_computation.4 | async-start | bytes 131072 | tf_op jit(solution)/shard_map/all_to_all | solution.py:222

commit v9 on v8

--- a/solution.py
+++ b/solution.py
@@ -60,6 +60,10 @@
 
 def kdot(left, right):
     return jnp.dot(left, right, precision=lax.Precision.HIGH, preferred_element_type=jnp.float32)
+
+
+def kdot_narrow(left, right):
+    return jnp.dot(left, right, preferred_element_type=jnp.float32)
 
 
 def split_taps(filt_spec, fr_ref, ff_ref, fm_ref):
@@ -100,8 +104,8 @@
     mixed = x_ref[:, 0, :, :].astype(jnp.float32).reshape(rows, tok)
     taps = x_ref[:, 1, :, :].astype(jnp.float32).reshape(rows, tok)
     table = fwd_ref[...]
-    spec_ref[...] = kdot(mixed, table)
-    filt_spec = kdot(taps, table)
+    spec_ref[...] = kdot_narrow(mixed, table)
+    filt_spec = kdot_narrow(taps, table)
     filt_ref[...] = filt_spec
     split_taps(filt_spec, fr_ref, ff_ref, fm_ref)
     pairs = [(out, [(out - lag, lag) for lag in range(out + 1)]) for out in range(blocks)]
@@ -117,7 +121,7 @@
     dconv = d_ref[...].astype(jnp.float32)
     fol_ref[: rows - chans, :] = dconv[chans:, :]
     fol_ref[rows - chans :, :] = jnp.zeros((chans, tok), jnp.float32)
-    spec_ref[...] = kdot(dconv, fwd_ref[:tok, :]) + kdot(fol_ref[...], fwd_ref[tok:, :])
+    spec_ref[...] = kdot_narrow(dconv, fwd_ref[:tok, :]) + kdot_narrow(fol_ref[...], fwd_ref[tok:, :])
     split_taps(filt_ref[...], fr_ref, ff_ref, fm_ref)
     pairs = [(out, [(out + lag, lag) for lag in range(blocks - out)]) for out in range(blocks)]
     block_terms(spec_ref, fr_ref, ff_ref, fm_ref, acc_ref, chans, pairs, True)

time: 85.8 us -> 85.3 us (level)
  no operation moved by 1% of the time
where the time goes in v9:
time: 85.3 us; the launch traced here: 84.8 us
  blocking collectives  51.5 us (60%)
  waiting for transfers between devices  11.6 us (14%)
  starting transfers between devices  9.67 us (11%)
  Pallas kernels  4.87 us (6%)
  local copies, waits for them, and re-layouts  4.84 us (6%)
  matrix products  1.22 us (1%)
    all_to_all x1, blocking collectives, chan_sum(): return jnp.sum(lax.all_to_all(spread, 'chan', 0, 0), axis=0)  21.1 us
    all_to_all x1, blocking collectives, body(): chan_in = lax.all_to_all(stacked, 'seq', 0, 0)  17.4 us
    all_to_all x1, blocking collectives, to_channels(): return lax.all_to_all(xt, 'seq', 0, 0)  13 us
    all_to_all x1, waiting for transfers between devices, from_channels(): back = lax.all_to_all(xc, 'seq', 0, 0)  6 us
    all_to_all x1, waiting for transfers between devices, body(): lax.all_to_all(dmixed_c.reshape(blocks, chans, tok), 'seq', 0, 0)  5.58 us
    all_to_all x1, starting transfers between devices, from_channels(): back = lax.all_to_all(xc, 'seq', 0, 0)  4.91 us
    pallas_call x2, Pallas kernels, vmem_call(): pl.pallas_call(kernel, out_shape=outs, in_specs=[pl.BlockSpec(memory_spac...  4.87 us
    unnamed x20, local copies, waits for them, and re-layouts  4.83 us
  transfers between devices with their start and end apart: 2, of which 2 were waited for; matrix products, arithmetic and copies ran while one was open for 3% of the time, Pallas kernels for 0%

profile of v9, /device:TPU:2, one launch (start us, length us, event | category | flops | bytes accessed | tf_op | source)
XLA Modules:
  0.0 84.8 jit_solution(7794276657544141945)
XLA Ops:
  0.6 0.0 copy-start
  0.6 0.0 copy-start.1
  0.7 0.0 copy-start.2
  0.7 0.8 copy-done
  1.5 0.2 convolution_convert_fusion
  1.7 0.0 copy-done.1
  1.7 0.0 copy-done.2
  1.7 0.2 convolution_convert_fusion.1
  1.9 17.4 %all_to_all.25.x_ref = bf16[16,2,16,128]{3,2,1,0:T(8,128)(2,1)} all-to-all(bf16[16,2,16,128]{3,2,1,0:T(8,128)(2,1)S(1)} %maximum_bitcast_fusion), channel_id=1, replica_groups=mesh['seq'=16,'chan'=32] {'seq'}, dimensions={0} | all-to-all | bytes 262144 | tf_op jit(solution)/shard_map/all_to_all | solution.py:180
  19.3 2.4 %shard_map.146 = (bf16[256,128]{1,0:T(8,128)(2,1)}, f32[256,256]{1,0:T(8,128)}) custom-call(bf16[16,2,16,128]{3,2,1,0:T(8,128)(2,1)} %all_to_all.25.x_ref, f32[128,256]{1,0:T(8,128)} %constant.16.clone.fwd_ref, f32[256,256]{1,0:T(8,128)} %constant.17.clone.inv_ref), custom_call_target="tpu_custom_call" | custom-call | tf_op jit(solution)/shard_map/pallas_call | solution.py:132
  21.8 0.0 copy-start.3
  21.8 4.9 %all-to-all-start.1 = ((bf16[16,16,128]{2,1,0:T(8,128)(2,1)}), bf16[16,16,128]{2,1,0:T(8,128)(2,1)S(1)}, u32[]{:S(2)}, u32[]{:S(2)}) async-start(bf16[16,16,128]{2,1,0:T(8,128)(2,1)} %bitcast.63), calls=%async_computation.1 | async-start | bytes 131072 | tf_op jit(solution)/shard_map/all_to_all | solution.py:150
  26.7 0.0 copy-done.3
  26.7 0.0 copy-start.4
  26.7 0.1 copy.27
  26.8 0.7 copy-done.4
  27.5 0.1 copy.26
  27.6 0.7 copy-done.5
  28.4 0.1 copy.28
  28.5 6.0 %all-to-all-done.1 = bf16[16,16,128]{2,1,0:T(8,128)(2,1)S(1)} async-done(((bf16[16,16,128]{2,1,0:T(8,128)(2,1)}), bf16[16,16,128]{2,1,0:T(8,128)(2,1)S(1)}, u32[]{:S(2)}, u32[]{:S(2)}) %all-to-all-start.1) | async-done | bytes 65568 | tf_op jit(solution)/shard_map/all_to_all | solution.py:150
  34.5 0.0 copy-done.6
  34.5 0.1 multiply_reduce_fusion.1
  34.6 21.1 %all_to_all.26 = f32[32,128,2]{1,2,0:T(2,128)S(1)} all-to-all(f32[32,128,2]{1,2,0:T(2,128)S(1)} %broadcast_in_dim.16), channel_id=1, replica_groups=mesh['seq'=16,'chan'=32] {'chan'}, dimensions={0} | all-to-all | bytes 65536 | tf_op jit(solution)/shard_map/all_to_all | solution.py:160
  55.8 0.1 fusion.2
  56.0 13.0 %all_to_all.27 = bf16[16,16,128]{2,1,0:T(8,128)(2,1)} all-to-all(bf16[16,16,128]{2,1,0:T(8,128)(2,1)S(1)} %bitcast.62), channel_id=1, replica_groups=mesh['seq'=16,'chan'=32] {'seq'}, dimensions={0} | all-to-all | bytes 131072 | tf_op jit(solution)/shard_map/all_to_all | solution.py:146
  68.9 2.5 %shard_map.147 = bf16[256,128]{1,0:T(8,128)(2,1)} custom-call(bf16[256,128]{1,0:T(8,128)(2,1)} %bitcast.61, f32[256,256]{1,0:T(8,128)} %get-tuple-element.8.filt_ref, f32[256,256]{1,0:T(8,128)} %constant.18.clone.fwd_ref, f32[256,128]{1,0:T(8,128)} %constant.19.clone.inv_ref), custom_call_target="tpu_custom_call" | custom-call | tf_op jit(solution)/shard_map/pallas_call | solution.py:132
  71.4 4.8 %all-to-all-start.4 = ((bf16[16,16,128]{2,1,0:T(8,128)(2,1)}), bf16[16,16,128]{2,1,0:T(8,128)(2,1)S(1)}, u32[]{:S(2)}, u32[]{:S(2)}) async-start(bf16[16,16,128]{2,1,0:T(8,128)(2,1)} %bitcast.60), calls=%async_computation.4 | async-start | bytes 131072 | tf_op jit(solution)/shard_map/all_to_all | solution.py:226
  76.1 0.7 copy.29
  76.9 0.7 copy.30
  77.6 0.7 copy.31
  78.4 5.6 %all-to-all-done.4 = bf16[16,16,128]{2,1,0:T(8,128)(2,1)S(1)} async-done(((bf16[16,16,128]{2,1,0:T(8,128)(2,1)}), bf16[16,16,128]{2,1,0:T(8,128)(2,1)S(1)}, u32[]{:S(2)}, u32[]{:S(2)}) %all-to-all-start.4) | async-done | bytes 65568 | tf_op jit(solution)/shard_map/all_to_all | solution.py:226
  83.9 0.9 %fusion.3 = (bf16[128,256]{1,0:T(8,128)(2,1)}, bf16[128,256]{1,0:T(8,128)(2,1)}) fusion(bf16[128,256]{1,0:T(8,128)(2,1)S(1)} %copy-done.2, bf16[128,256]{1,0:T(8,128)(2,1)S(1)} %copy-done.1, bf16[256,128]{1,0:T(8,128)(2,1)S(1)} %bitcast.59), kind=kOutput, calls=%fused_computation.11 | convolution fusion | flops 17039360 | bytes 327680 | tf_op jit(solution)/shard_map/dot_general | solution.py:227
  (7 shorter events, 0.1 us)
Async XLA Ops:
  0.6 0.8 copy-start
  0.6 1.0 %copy-start.1 = (bf16[128,256]{1,0:T(8,128)(2,1)S(1)}, bf16[128,256]{1,0:T(8,128)(2,1)}, u32[]{:S(2)}) copy-start(bf16[128,256]{1,0:T(8,128)(2,1)} %param.14) | copy-start | bytes 196612
  0.7 1.0 %copy-start.2 = (bf16[128,256]{1,0:T(8,128)(2,1)S(1)}, bf16[128,256]{1,0:T(8,128)(2,1)}, u32[]{:S(2)}) copy-start(bf16[128,256]{1,0:T(8,128)(2,1)} %param.13) | copy-start | bytes 196612
  21.8 4.9 %copy-start.3 = (bf16[128,256]{1,0:T(8,128)(2,1)S(1)}, bf16[128,256]{1,0:T(8,128)(2,1)}, u32[]{:S(2)}) copy-start(bf16[128,256]{1,0:T(8,128)(2,1)} %param.12) | copy-start | bytes 196612
  21.8 12.7 %all-to-all-start.1 = ((bf16[16,16,128]{2,1,0:T(8,128)(2,1)}), bf16[16,16,128]{2,1,0:T(8,128)(2,1)S(1)}, u32[]{:S(2)}, u32[]{:S(2)}) async-start(bf16[16,16,128]{2,1,0:T(8,128)(2,1)} %bitcast.63), calls=%async_computation.1 | async-start | bytes 131072 | tf_op jit(solution)/shard_map/all_to_all | solution.py:150
  26.7 0.8 copy-start.4
  27.5 0.8 copy-start.5
  28.4 6.1 %copy-start.6 = (f32[256]{0:T(256)S(1)}, f32[256]{0:T(256)}, u32[]{:S(2)}) copy-start(f32[256]{0:T(256)} %param.16) | copy-start | bytes 3076
  71.4 12.6 %all-to-all-start.4 = ((bf16[16,16,128]{2,1,0:T(8,128)(2,1)}), bf16[16,16,128]{2,1,0:T(8,128)(2,1)S(1)}, u32[]{:S(2)}, u32[]{:S(2)}) async-start(bf16[16,16,128]{2,1,0:T(8,128)(2,1)} %bitcast.60), calls=%async_computation.4 | async-start | bytes 131072 | tf_op jit(solution)/shard_map/all_to_all | solution.py:226
